TPU v7x, 512 devices: a whole 4x4x16 slice. The times are simulated.
512 devices in a mesh: dp: 64 (over z, x), tensor: 8 (over y, core).
Axes of the slice: x: 4, y: 4, z: 16, core: 2. Of those that a mesh axis runs over, the one named last changes fastest.
Arguments:
- queries: bfloat16 [8192, 8192], P('dp', 'tensor'), may hold values from -160 to 160, as said below
- key_cache_table: bfloat16 [8192, 32, 1024], P('dp', None, 'tensor'), may hold values from -4.5 to 4.5, as said below
- value_cache_table: bfloat16 [8192, 32, 1024], P('dp', None, 'tensor'), may hold values from -6 to 6
- filled_lengths: int32 [8192], P('dp'), may hold values from 8 to 32, as said below
- request_adapter: int32 [8192], replicated, may hold values from 0 to 1023, as said below
- adapter_store_row: int32 [1024], replicated, may hold values from 0 to 1023, as said below
- adapter_factor: float32 [1024], replicated, may hold values from 1 to 8
- adapter_down_store: bfloat16 [1024, 16, 8192], P('dp', None, 'tensor'), may hold values from -0.0625 to 0.0625
- adapter_up_store: bfloat16 [1024, 16, 8192], P('dp', None, 'tensor'), may hold values from -1.5 to 1.5
Outputs:
- attended: bfloat16 [8192, 8192], P('dp', 'tensor')
- adapter_delta: bfloat16 [8192, 8192], P('dp', 'tensor')
Inputs may be any that keep to these rules, and one draw needn't show every extreme that they name: A custom draw; in the hidden draw some queries are aligned with keys of the same request. `key_cache_table`: A custom draw. `filled_lengths`: some request has all 32 slots filled. A permutation: adapter a is held by store shard adapter_store_row[a] // 16. `request_adapter`: in each aligned block of 128 requests (one group), at most 4 requests name adapters held by one store shard; every group reaches 4 for some shard, and one shard receives 4 from every group.
All inputs are finite; a program needn't handle non-finite values.
Results may differ from a plain program's by a relative error of at most 0.0064.
Values may be sent and summed in bfloat16 or wider, within the bound.
No kernel may reach another device: no remote copies, remote signals or barrier semaphores. Data moves between devices by JAX's collectives and lax.ppermute only.
A program may use at most 128 MiB of HBM per device.

v0:
```python
import math

import jax
import jax.numpy as jnp
from jax import lax
from jax.sharding import PartitionSpec as P

HEAD_WIDTH = 128


def from_everyone(value, axis):
    copies = jnp.broadcast_to(value, (lax.axis_size(axis), *value.shape))
    return lax.all_to_all(copies, axis, split_axis=0, concat_axis=0, tiled=True)


def of_everyone(value, axis):
    return from_everyone(value, axis).sum(axis=0)


def body(
    queries,
    key_cache_table,
    value_cache_table,
    filled_lengths,
    request_adapter,
    adapter_store_row,
    adapter_factor,
    adapter_down_store,
    adapter_up_store,
):
    requests = queries.shape[0]
    row_width = queries.shape[1]
    kv_local = key_cache_table.shape[2] // HEAD_WIDTH
    heads_local = row_width // HEAD_WIDTH
    group_width = heads_local // kv_local
    length = key_cache_table.shape[1]
    highest = lax.Precision.HIGHEST
    heads_of_query = queries.reshape(requests, kv_local, group_width, HEAD_WIDTH)
    heads_of_key = key_cache_table.reshape(requests, length, kv_local, HEAD_WIDTH)
    heads_of_value = value_cache_table.reshape(requests, length, kv_local, HEAD_WIDTH)
    scores = jnp.einsum(
        "bkgd,blkd->bkgl", heads_of_query, heads_of_key, preferred_element_type=jnp.float32
    ) * (1.0 / math.sqrt(HEAD_WIDTH))
    visible = (jnp.arange(length)[None, :] < filled_lengths[:, None])[:, None, None, :]
    scores = jnp.where(visible, scores, jnp.float32(-1e30))
    row_max = jnp.max(scores, axis=-1, keepdims=True)
    exp_scores = jnp.exp(scores - row_max)
    weights = (exp_scores / jnp.sum(exp_scores, axis=-1, keepdims=True)).astype(jnp.bfloat16)
    attended = jnp.einsum(
        "bkgl,blkd->bkgd", weights, heads_of_value, preferred_element_type=jnp.float32
    )
    attended = attended.astype(jnp.bfloat16).reshape(requests, row_width)
    group_count = lax.axis_size("dp")
    capacity = max(2, 2 * requests // group_count)
    slot_count = group_count * capacity
    stored_total = adapter_down_store.shape[0]
    rank_width = adapter_down_store.shape[1]
    adapter_count = adapter_store_row.shape[0]
    high_count = adapter_count // stored_total
    group_index = lax.axis_index("dp")
    owner_values = (adapter_store_row // stored_total).astype(jnp.float32)
    slot_values = (adapter_store_row % stored_total).astype(jnp.float32)
    table_stack = jnp.stack([owner_values, slot_values, adapter_factor], axis=0).reshape(
        3, high_count, stored_total
    )
    id_table = request_adapter.reshape(group_count, requests)
    id_high = id_table // stored_total
    id_low = id_table % stored_total
    high_hot = (id_high[:, :, None] == jnp.arange(high_count)[None, None, :]).astype(jnp.float32)
    low_hot = (id_low[:, :, None] == jnp.arange(stored_total)[None, None, :]).astype(jnp.float32)
    row_pick = jnp.einsum("grh,chl->cgrl", high_hot, table_stack, precision=highest)
    looked = jnp.sum(row_pick * low_hot[None], axis=-1)
    owner_shard = looked[0].astype(jnp.int32)
    store_slot = looked[1].astype(jnp.int32)
    scale_table = looked[2]
    owner_hot = (owner_shard[:, :, None] == jnp.arange(group_count)[None, None, :]).astype(
        jnp.float32
    )
    earlier = (jnp.arange(requests)[:, None] > jnp.arange(requests)[None, :]).astype(jnp.float32)
    before = jnp.einsum("ij,gjs->gis", earlier, owner_hot, precision=highest)
    order_in = jnp.sum(before * owner_hot, axis=-1)
    cell_index = owner_shard.astype(jnp.float32) * capacity + order_in
    my_cell = lax.dynamic_index_in_dim(cell_index, group_index, 0, keepdims=False)
    slot_iota = jnp.arange(slot_count).astype(jnp.float32)
    chosen_mask = (my_cell[:, None] == slot_iota[None, :]).astype(jnp.float32)
    chosen = chosen_mask.astype(jnp.bfloat16)
    matches = (
        (owner_shard == group_index)[:, :, None]
        & (order_in[:, :, None] == jnp.arange(capacity).astype(jnp.float32)[None, None, :])
    ).astype(jnp.float32)
    slot_hot = (store_slot[:, :, None] == jnp.arange(stored_total)[None, None, :]).astype(
        jnp.float32
    )
    picked = jnp.einsum("grc,gra->gca", matches, slot_hot, precision=highest)
    item_scale = jnp.einsum("grc,gr->gc", matches, scale_table, precision=highest)
    chosen_back = (slot_iota[:, None] == my_cell[None, :]).astype(jnp.bfloat16)
    outgoing = jnp.dot(chosen_back, attended, preferred_element_type=jnp.float32).astype(
        jnp.bfloat16
    )
    arrived = lax.all_to_all(
        outgoing.reshape(group_count, capacity, row_width),
        "dp",
        split_axis=0,
        concat_axis=0,
        tiled=True,
    )
    flat_rows = arrived.reshape(slot_count, row_width)
    store_down = adapter_down_store.reshape(stored_total * rank_width, row_width)
    products = lax.dot_general(
        flat_rows, store_down, (((1,), (1,)), ((), ())), preferred_element_type=jnp.float32
    )
    picked_flat = picked.reshape(slot_count, stored_total)
    partial_value = jnp.sum(
        products.reshape(slot_count, stored_total, rank_width) * picked_flat[:, :, None], axis=1
    )
    summed = of_everyone(partial_value, "tensor")
    low_rank = (summed * item_scale.reshape(slot_count)[:, None]).astype(jnp.bfloat16)
    spread = (picked_flat.astype(jnp.bfloat16)[:, :, None] * low_rank[:, None, :]).reshape(
        slot_count, stored_total * rank_width
    )
    store_up = adapter_up_store.reshape(stored_total * rank_width, row_width)
    result = jnp.dot(spread, store_up, preferred_element_type=jnp.float32).astype(jnp.bfloat16)
    returned = lax.all_to_all(
        result.reshape(group_count, capacity, row_width),
        "dp",
        split_axis=0,
        concat_axis=0,
        tiled=True,
    )
    adapter_delta = jnp.dot(
        chosen, returned.reshape(slot_count, row_width), preferred_element_type=jnp.float32
    ).astype(jnp.bfloat16)
    return (attended, adapter_delta)


def solution(mesh):
    placed = (
        P("dp", "tensor"),
        P("dp", None, "tensor"),
        P("dp", None, "tensor"),
        P("dp"),
        P(),
        P(),
        P(),
        P("dp", None, "tensor"),
        P("dp", None, "tensor"),
    )
    return jax.shard_map(
        body,
        mesh=mesh,
        in_specs=placed,
        out_specs=(P("dp", "tensor"), P("dp", "tensor")),
        check_vma=False,
    )
```

profile of v0, /device:TPU:6, one launch (start us, length us, event | category | flops | bytes accessed | tf_op | source)
XLA Modules:
  0.0 115.5 jit_solution(11646651353620882095)
XLA Ops:
  0.6 0.0 copy-start
  0.7 0.8 fusion.46
  1.4 0.7 iota_compare_fusion.9
  2.2 0.1 stack.12
  2.3 0.1 copy.16
  2.3 0.1 stack.13
  2.4 0.1 copy.17
  2.5 0.8 stack.14
  3.3 0.1 copy.18
  3.3 0.8 add_select_fusion
  4.1 1.0 copy.24
  5.1 1.9 %fusion.11 = f32[128,8,32]{2,1,0:T(8,128)S(1)} fusion(bf16[128,8,128]{2,1,0:T(8,128)(2,1)S(1)} %bitcast.83, bf16[128,32,128]{2,1,0:T(8,128)(2,1)} %param.10, pred[128,32]{1,0:T(8,128)(4,1)S(1)} %iota_compare_fusion.9), kind=kOutput, calls=%fused_computation.15 | convolution fusion | flops 8454144 | bytes 1445888 | tf_op jit(solution)/shard_map/bkgd,blkd->bkgl/dot_general | solution.py:41
  7.0 0.4 fusion.54
  7.4 0.0 copy-done
  7.4 1.9 %convolution_convert_fusion.2 = bf16[128,8,128]{2,1,0:T(8,128)(2,1)S(1)} fusion(bf16[128,32,128]{2,1,0:T(8,128)(2,1)S(1)} %copy-done, f32[128,8]{1,0:T(8,128)S(1)} %fusion.54, f32[128,8,32]{2,1,0:T(8,128)S(1)} %fusion.11), kind=kOutput, calls=%fused_computation.18 | convolution fusion | flops 8619039 | bytes 1445888 | tf_op jit(solution)/shard_map/bkgl,blkd->bkgd/dot_general | solution.py:49
  9.3 0.1 copy.27
  9.3 0.0 copy-start.1
  9.4 1.1 fusion.6
  10.5 0.7 fusion.1
  11.2 0.0 copy-done.1
  11.2 0.3 convolution_convert_fusion
  11.5 1.0 reshape.202
  12.5 18.6 %all-to-all-start = ((bf16[64,4,1024]{2,1,0:T(4,128)(2,1)}), bf16[64,4,1024]{2,1,0:T(4,128)(2,1)S(1)}, u32[]{:S(2)}, u32[]{:S(2)}) async-start(bf16[64,4,1024]{2,1,0:T(4,128)(2,1)} %reshape.202), calls=%async_computation | async-start | bytes 1048576 | tf_op jit(solution)/shard_map/all_to_all | solution.py:100
  31.1 0.0 copy-start.2
  31.1 0.3 fusion.17
  31.4 0.1 copy.20
  31.5 32.3 %all-to-all-done = bf16[64,4,1024]{2,1,0:T(4,128)(2,1)S(1)} async-done(((bf16[64,4,1024]{2,1,0:T(4,128)(2,1)}), bf16[64,4,1024]{2,1,0:T(4,128)(2,1)S(1)}, u32[]{:S(2)}, u32[]{:S(2)}) %all-to-all-start) | async-done | bytes 524320 | tf_op jit(solution)/shard_map/all_to_all | solution.py:100
  63.8 0.1 reshape.209
  63.9 0.0 copy-done.2
  64.0 0.0 copy-start.3
  64.0 0.3 fusion.13
  64.3 0.7 broadcast_in_dim.16
  65.0 4.5 %all-to-all-start.1 = ((f32[8,256,16]{1,2,0:T(8,128)}), f32[8,256,16]{1,2,0:T(8,128)S(1)}, u32[]{:S(2)}, u32[]{:S(2)}) async-start(f32[8,256,16]{1,2,0:T(8,128)} %broadcast_in_dim.16), calls=%async_computation.1 | async-start | bytes 262144 | tf_op jit(solution)/shard_map/all_to_all | solution.py:13
  69.5 0.4 fusion.22
  69.9 0.1 mul.69
  70.0 0.1 copy.19
  70.0 5.5 %all-to-all-done.1 = f32[8,256,16]{1,2,0:T(8,128)S(1)} async-done(((f32[8,256,16]{1,2,0:T(8,128)}), f32[8,256,16]{1,2,0:T(8,128)S(1)}, u32[]{:S(2)}, u32[]{:S(2)}) %all-to-all-start.1) | async-done | bytes 131104 | tf_op jit(solution)/shard_map/all_to_all | solution.py:13
  75.6 0.0 copy-done.3
  75.6 0.3 fusion.9
  76.0 0.2 reshape.204
  76.2 38.3 %all_to_all.15 = bf16[64,4,1024]{2,1,0:T(4,128)(2,1)S(1)} all-to-all(bf16[64,4,1024]{2,1,0:T(4,128)(2,1)S(1)} %reshape.204), channel_id=1, replica_groups=mesh['dp'=64,'tensor'=8] {'dp'}, dimensions={0} | all-to-all | bytes 1048576 | tf_op jit(solution)/shard_map/all_to_all | solution.py:123
  114.4 0.1 reshape.205
  114.6 1.0 convolution_convert_fusion.1
  (9 shorter events, 0.1 us)
Async XLA Ops:
  0.6 6.7 %copy-start = (bf16[128,32,128]{2,1,0:T(8,128)(2,1)S(1)}, bf16[128,32,128]{2,1,0:T(8,128)(2,1)}, u32[]{:S(2)}) copy-start(bf16[128,32,128]{2,1,0:T(8,128)(2,1)} %param.11) | copy-start | bytes 3145732
  9.3 1.9 %copy-start.1 = (bf16[16,8,8,128]{3,1,2,0:T(8,128)(2,1)}, bf16[16,8,8,128]{3,1,2,0:T(8,128)(2,1)S(1)}, u32[]{:S(2)}) copy-start(bf16[16,8,8,128]{3,1,2,0:T(8,128)(2,1)S(1)} %copy.27) | copy-start | bytes 786436
  12.5 51.3 %all-to-all-start = ((bf16[64,4,1024]{2,1,0:T(4,128)(2,1)}), bf16[64,4,1024]{2,1,0:T(4,128)(2,1)S(1)}, u32[]{:S(2)}, u32[]{:S(2)}) async-start(bf16[64,4,1024]{2,1,0:T(4,128)(2,1)} %reshape.202), calls=%async_computation | async-start | bytes 1048576 | tf_op jit(solution)/shard_map/all_to_all | solution.py:100
  31.1 32.8 %copy-start.2 = (bf16[16,16,1024]{2,1,0:T(8,128)(2,1)S(1)}, bf16[16,16,1024]{2,1,0:T(8,128)(2,1)}, u32[]{:S(2)}) copy-start(bf16[16,16,1024]{2,1,0:T(8,128)(2,1)} %param.16) | copy-start | bytes 1572868
  64.0 11.7 %copy-start.3 = (bf16[16,16,1024]{2,1,0:T(8,128)(2,1)S(1)}, bf16[16,16,1024]{2,1,0:T(8,128)(2,1)}, u32[]{:S(2)}) copy-start(bf16[16,16,1024]{2,1,0:T(8,128)(2,1)} %param.17) | copy-start | bytes 1572868
  65.0 10.6 %all-to-all-start.1 = ((f32[8,256,16]{1,2,0:T(8,128)}), f32[8,256,16]{1,2,0:T(8,128)S(1)}, u32[]{:S(2)}, u32[]{:S(2)}) async-start(f32[8,256,16]{1,2,0:T(8,128)} %broadcast_in_dim.16), calls=%async_computation.1 | async-start | bytes 262144 | tf_op jit(solution)/shard_map/all_to_all | solution.py:13
where the time goes:
time: 116 us
  blocking collectives  38.3 us (33%)
  waiting for transfers between devices  37.8 us (33%)
  starting transfers between devices  23.1 us (20%)
  matrix products  8.18 us (7%)
  local copies, waits for them, and re-layouts  4.53 us (4%)
  other arithmetic  2.8 us (2%)
    all_to_all x1, blocking collectives, body(): lax.all_to_all(result.reshape(group_count, capacity, row_width), 'dp', sp...  38.3 us
    all_to_all x1, waiting for transfers between devices, body(): lax.all_to_all(outgoing.reshape(group_count, capacity, row_width), 'dp',...  32.3 us
    all_to_all x1, starting transfers between devices, body(): lax.all_to_all(outgoing.reshape(group_count, capacity, row_width), 'dp',...  18.6 us
    all_to_all x1, waiting for transfers between devices, from_everyone(): return lax.all_to_all(copies, axis, split_axis=0, concat_axis=0, tiled=True)  5.55 us
    all_to_all x1, starting transfers between devices, from_everyone(): return lax.all_to_all(copies, axis, split_axis=0, concat_axis=0, tiled=True)  4.47 us
  transfers between devices with their start and end apart: 2, of which 2 were waited for; matrix products, arithmetic and copies ran while one was open for 1% of the time, Pallas kernels for 0%

commit v1 on v0

v1 whole, which is shorter than its diff:
```python
import math

import jax
import jax.numpy as jnp
from jax import lax
from jax.sharding import PartitionSpec as P

HEAD_WIDTH = 128


def of_everyone(value, axis):
    copies = jnp.broadcast_to(value, (lax.axis_size(axis), *value.shape))
    return lax.all_to_all(copies, axis, split_axis=0, concat_axis=0, tiled=True).sum(axis=0)


def attention(queries, key_cache_table, value_cache_table, filled_lengths):
    requests, row_width = queries.shape
    kv_local = key_cache_table.shape[2] // HEAD_WIDTH
    group_width = row_width // HEAD_WIDTH // kv_local
    length = key_cache_table.shape[1]
    heads_of_query = queries.reshape(requests, kv_local, group_width, HEAD_WIDTH)
    heads_of_key = key_cache_table.reshape(requests, length, kv_local, HEAD_WIDTH)
    heads_of_value = value_cache_table.reshape(requests, length, kv_local, HEAD_WIDTH)
    scores = jnp.einsum(
        "bkgd,blkd->bkgl", heads_of_query, heads_of_key, preferred_element_type=jnp.float32
    ) * (1.0 / math.sqrt(HEAD_WIDTH))
    visible = (jnp.arange(length)[None, :] < filled_lengths[:, None])[:, None, None, :]
    scores = jnp.where(visible, scores, jnp.float32(-1e30))
    row_max = jnp.max(scores, axis=-1, keepdims=True)
    exp_scores = jnp.exp(scores - row_max)
    weights = (exp_scores / jnp.sum(exp_scores, axis=-1, keepdims=True)).astype(jnp.bfloat16)
    attended = jnp.einsum(
        "bkgl,blkd->bkgd", weights, heads_of_value, preferred_element_type=jnp.float32
    )
    return attended.astype(jnp.bfloat16).reshape(requests, row_width)


def prefix_count(mask):
    n = mask.shape[-1]
    earlier = (jnp.arange(n)[:, None] < jnp.arange(n)[None, :]).astype(jnp.bfloat16)
    return jnp.einsum(
        "...i,ij->...j", mask.astype(jnp.bfloat16), earlier, preferred_element_type=jnp.float32
    )


def body(
    queries,
    key_cache_table,
    value_cache_table,
    filled_lengths,
    request_adapter,
    adapter_store_row,
    adapter_factor,
    adapter_down_store,
    adapter_up_store,
):
    requests, row_width = queries.shape
    group_count = lax.axis_size("dp")
    group_index = lax.axis_index("dp")
    capacity = max(2, 2 * requests // group_count)
    slot_count = group_count * capacity
    stored_total, rank_width = adapter_down_store.shape[0], adapter_down_store.shape[1]
    adapter_count = adapter_store_row.shape[0]

    attended = attention(queries, key_cache_table, value_cache_table, filled_lengths)

    own_ids = lax.dynamic_slice_in_dim(request_adapter, group_index * requests, requests)
    id_hot = own_ids[:, None] == jnp.arange(adapter_count)[None, :]
    own_row = jnp.sum(jnp.where(id_hot, adapter_store_row[None, :], 0), axis=1)
    own_dest = own_row // stored_total
    same_dest = own_dest[:, None] == own_dest[None, :]
    before = jnp.arange(requests)[:, None] > jnp.arange(requests)[None, :]
    own_order = jnp.sum((same_dest & before).astype(jnp.int32), axis=1)
    own_cell = own_dest * capacity + own_order
    cell_hot = own_cell[None, :] == jnp.arange(slot_count)[:, None]
    outgoing = jnp.einsum(
        "cb,bf->cf", cell_hot.astype(jnp.bfloat16), attended, preferred_element_type=jnp.float32
    ).astype(jnp.bfloat16)
    arrived = lax.all_to_all(
        outgoing.reshape(group_count, capacity, row_width), "dp", 0, 0, tiled=True
    ).reshape(slot_count, row_width)

    local_rows = group_index * stored_total + jnp.arange(stored_total)
    holds = adapter_store_row[None, :] == local_rows[:, None]
    local_ids = jnp.sum(jnp.where(holds, jnp.arange(adapter_count)[None, :], 0), axis=1)
    local_factor = jnp.sum(jnp.where(holds, adapter_factor[None, :], 0.0), axis=1)
    all_ids = request_adapter.reshape(group_count, requests)
    hit = (all_ids[:, :, None] == local_ids[None, None, :]).astype(jnp.bfloat16)
    mine = jnp.sum(hit, axis=2)
    order_in = prefix_count(mine)
    pick = (mine[:, None, :] > 0) & (
        order_in[:, None, :] == jnp.arange(capacity, dtype=jnp.float32)[None, :, None]
    )
    picked = jnp.einsum(
        "gcb,gbj->gcj", pick.astype(jnp.bfloat16), hit, preferred_element_type=jnp.float32
    ).reshape(slot_count, stored_total)
    item_scale = jnp.dot(picked, local_factor, precision=lax.Precision.HIGHEST)

    store_down = adapter_down_store.reshape(stored_total * rank_width, row_width)
    products = lax.dot_general(
        arrived, store_down, (((1,), (1,)), ((), ())), preferred_element_type=jnp.float32
    )
    partial_value = jnp.sum(
        products.reshape(slot_count, stored_total, rank_width) * picked[:, :, None], axis=1
    )
    summed = of_everyone(partial_value, "tensor")
    low_rank = (summed * item_scale[:, None]).astype(jnp.bfloat16)
    spread = (picked.astype(jnp.bfloat16)[:, :, None] * low_rank[:, None, :]).reshape(
        slot_count, stored_total * rank_width
    )
    store_up = adapter_up_store.reshape(stored_total * rank_width, row_width)
    result = jnp.dot(spread, store_up, preferred_element_type=jnp.float32).astype(jnp.bfloat16)
    returned = lax.all_to_all(
        result.reshape(group_count, capacity, row_width), "dp", 0, 0, tiled=True
    ).reshape(slot_count, row_width)
    adapter_delta = jnp.einsum(
        "cb,cf->bf", cell_hot.astype(jnp.bfloat16), returned, preferred_element_type=jnp.float32
    ).astype(jnp.bfloat16)
    return (attended, adapter_delta)


def solution(mesh):
    placed = (
        P("dp", "tensor"),
        P("dp", None, "tensor"),
        P("dp", None, "tensor"),
        P("dp"),
        P(),
        P(),
        P(),
        P("dp", None, "tensor"),
        P("dp", None, "tensor"),
    )
    return jax.shard_map(
        body,
        mesh=mesh,
        in_specs=placed,
        out_specs=(P("dp", "tensor"), P("dp", "tensor")),
        check_vma=False,
    )
```

time: 116 us -> 113 us (0.974)
  matrix products: 8.18 us -> 6.32 us
  other arithmetic: 2.8 us -> 1.45 us
    dot_general x9 -> x8, matrix products: 7.86 us -> 6 us  [the longest x1 1.89 us: attention(): jnp.einsum('bkgl,blkd->bkgd', weights, heads_of_value, preferred_element_...]
    all_to_all x1, waiting for transfers between devices: 32.3 us -> 30.9 us  [body(): lax.all_to_all(outgoing.reshape(group_count, capacity, row_width), 'dp',...]
where the time goes in v1:
time: 113 us; the launch traced here: 112 us
  blocking collectives  38.3 us (34%)
  waiting for transfers between devices  36.8 us (33%)
  starting transfers between devices  23.2 us (21%)
  matrix products  6.32 us (6%)
  local copies, waits for them, and re-layouts  5.18 us (5%)
  other arithmetic  1.45 us (1%)
    all_to_all x1, blocking collectives, body(): lax.all_to_all(result.reshape(group_count, capacity, row_width), 'dp', 0,...  38.3 us
    all_to_all x1, waiting for transfers between devices, body(): lax.all_to_all(outgoing.reshape(group_count, capacity, row_width), 'dp',...  30.9 us
    all_to_all x1, starting transfers between devices, body(): lax.all_to_all(outgoing.reshape(group_count, capacity, row_width), 'dp',...  18.7 us
    all_to_all x1, waiting for transfers between devices, of_everyone(): lax.all_to_all(copies, axis, split_axis=0, concat_axis=0, tiled=True)  5.96 us
    all_to_all x1, starting transfers between devices, of_everyone(): lax.all_to_all(copies, axis, split_axis=0, concat_axis=0, tiled=True)  4.47 us
  transfers between devices with their start and end apart: 2, of which 2 were waited for; matrix products, arithmetic and copies ran while one was open for 1% of the time, Pallas kernels for 0%

profile of v1, /device:TPU:6, one launch (start us, length us, event | category | flops | bytes accessed | tf_op | source)
XLA Modules:
  0.0 112.1 jit_solution(15202753013062365391)
XLA Ops:
  0.6 0.0 copy-start
  0.7 0.0 copy-start.2
  0.7 0.9 dynamic_slice.3
  1.5 0.0 copy-done.2
  1.5 0.2 select_reduce_fusion
  1.7 0.2 convert_reduce_fusion
  1.9 0.0 copy-start.5
  1.9 1.0 copy.15
  2.9 0.0 copy-done.5
  3.0 0.1 iota_compare_fusion.7
  3.0 1.9 %fusion.3 = f32[128,8,32]{2,1,0:T(8,128)S(1)} fusion(bf16[128,8,128]{2,1,0:T(8,128)(2,1)S(1)} %bitcast.31, bf16[128,32,128]{2,1,0:T(8,128)(2,1)} %param.10, pred[128,32]{1,0:T(8,128)(4,1)S(1)} %iota_compare_fusion.7), kind=kOutput, calls=%fused_computation.6 | convolution fusion | flops 8454144 | bytes 1445888 | tf_op jit(solution)/shard_map/bkgd,blkd->bkgl/dot_general | solution.py:24
  4.9 0.4 fusion.27
  5.3 0.0 copy-done
  5.3 1.9 %convolution_convert_fusion.2 = bf16[128,8,128]{2,1,0:T(8,128)(2,1)S(1)} fusion(bf16[128,32,128]{2,1,0:T(8,128)(2,1)S(1)} %copy-done, f32[128,8]{1,0:T(8,128)S(1)} %fusion.27, f32[128,8,32]{2,1,0:T(8,128)S(1)} %fusion.3), kind=kOutput, calls=%fused_computation.9 | convolution fusion | flops 8619039 | bytes 1445888 | tf_op jit(solution)/shard_map/bkgl,blkd->bkgd/dot_general | solution.py:32
  7.2 0.1 copy.18
  7.2 0.0 copy-start.1
  7.3 0.3 convolution_convert_fusion
  7.6 0.4 copy-done.1
  8.0 1.0 reshape.158
  8.9 0.0 copy-start.3
  8.9 18.7 %all-to-all-start = ((bf16[64,4,1024]{2,1,0:T(4,128)(2,1)}), bf16[64,4,1024]{2,1,0:T(4,128)(2,1)S(1)}, u32[]{:S(2)}, u32[]{:S(2)}) async-start(bf16[64,4,1024]{2,1,0:T(4,128)(2,1)} %reshape.158), calls=%async_computation | async-start | bytes 1048576 | tf_op jit(solution)/shard_map/all_to_all | solution.py:79
  27.7 0.2 fusion.15
  27.9 0.0 copy-done.3
  27.9 0.2 fusion.8
  28.1 0.1 fusion.23
  28.2 0.3 fusion.6
  28.5 0.1 copy.14
  28.6 0.0 copy-start.4
  28.6 0.1 copy.13
  28.7 0.6 copy-done.4
  29.3 0.2 fusion.16
  29.5 0.0 copy-start.6
  29.5 30.9 %all-to-all-done = bf16[64,4,1024]{2,1,0:T(4,128)(2,1)S(1)} async-done(((bf16[64,4,1024]{2,1,0:T(4,128)(2,1)}), bf16[64,4,1024]{2,1,0:T(4,128)(2,1)S(1)}, u32[]{:S(2)}, u32[]{:S(2)}) %all-to-all-start) | async-done | bytes 524320 | tf_op jit(solution)/shard_map/all_to_all | solution.py:79
  60.4 0.1 reshape.162
  60.5 0.0 copy-done.6
  60.5 0.3 fusion.5
  60.9 0.0 copy-start.7
  60.9 0.7 broadcast_in_dim.56
  61.5 4.5 %all-to-all-start.1 = ((f32[8,256,16]{1,2,0:T(8,128)}), f32[8,256,16]{1,2,0:T(8,128)S(1)}, u32[]{:S(2)}, u32[]{:S(2)}) async-start(f32[8,256,16]{1,2,0:T(8,128)} %broadcast_in_dim.56), calls=%async_computation.1 | async-start | bytes 262144 | tf_op jit(solution)/shard_map/all_to_all | solution.py:13
  66.0 0.2 fusion.25
  66.2 6.0 %all-to-all-done.1 = f32[8,256,16]{1,2,0:T(8,128)S(1)} async-done(((f32[8,256,16]{1,2,0:T(8,128)}), f32[8,256,16]{1,2,0:T(8,128)S(1)}, u32[]{:S(2)}, u32[]{:S(2)}) %all-to-all-start.1) | async-done | bytes 131104 | tf_op jit(solution)/shard_map/all_to_all | solution.py:13
  72.2 0.0 copy-done.7
  72.2 0.3 fusion.1
  72.5 0.2 reshape.160
  72.7 38.3 %all_to_all.15 = bf16[64,4,1024]{2,1,0:T(4,128)(2,1)S(1)} all-to-all(bf16[64,4,1024]{2,1,0:T(4,128)(2,1)S(1)} %reshape.160), channel_id=1, replica_groups=mesh['dp'=64,'tensor'=8] {'dp'}, dimensions={0} | all-to-all | bytes 1048576 | tf_op jit(solution)/shard_map/all_to_all | solution.py:113
  111.0 0.1 reshape.161
  111.1 1.0 convolution_convert_fusion.1
  (7 shorter events, 0.1 us)
Async XLA Ops:
  0.6 4.7 %copy-start = (bf16[128,32,128]{2,1,0:T(8,128)(2,1)S(1)}, bf16[128,32,128]{2,1,0:T(8,128)(2,1)}, u32[]{:S(2)}) copy-start(bf16[128,32,128]{2,1,0:T(8,128)(2,1)} %param.11) | copy-start | bytes 3145732
  0.7 0.9 copy-start.2
  1.9 1.0 copy-start.5
  7.2 0.7 copy-start.1
  8.9 18.9 %copy-start.3 = (s32[8192]{0:T(1024)S(1)}, s32[8192]{0:T(1024)}, u32[]{:S(2)}) copy-start(s32[8192]{0:T(1024)} %param.13) | copy-start | bytes 98308
  8.9 51.4 %all-to-all-start = ((bf16[64,4,1024]{2,1,0:T(4,128)(2,1)}), bf16[64,4,1024]{2,1,0:T(4,128)(2,1)S(1)}, u32[]{:S(2)}, u32[]{:S(2)}) async-start(bf16[64,4,1024]{2,1,0:T(4,128)(2,1)} %reshape.158), calls=%async_computation | async-start | bytes 1048576 | tf_op jit(solution)/shard_map/all_to_all | solution.py:79
  28.6 0.7 copy-start.4
  29.5 31.0 %copy-start.6 = (bf16[16,16,1024]{2,1,0:T(8,128)(2,1)S(1)}, bf16[16,16,1024]{2,1,0:T(8,128)(2,1)}, u32[]{:S(2)}) copy-start(bf16[16,16,1024]{2,1,0:T(8,128)(2,1)} %param.16) | copy-start | bytes 1572868
  60.9 11.3 %copy-start.7 = (bf16[16,16,1024]{2,1,0:T(8,128)(2,1)S(1)}, bf16[16,16,1024]{2,1,0:T(8,128)(2,1)}, u32[]{:S(2)}) copy-start(bf16[16,16,1024]{2,1,0:T(8,128)(2,1)} %param.17) | copy-start | bytes 1572868
  61.5 10.6 %all-to-all-start.1 = ((f32[8,256,16]{1,2,0:T(8,128)}), f32[8,256,16]{1,2,0:T(8,128)S(1)}, u32[]{:S(2)}, u32[]{:S(2)}) async-start(f32[8,256,16]{1,2,0:T(8,128)} %broadcast_in_dim.56), calls=%async_computation.1 | async-start | bytes 262144 | tf_op jit(solution)/shard_map/all_to_all | solution.py:13

commit v2 on v1

--- a/solution.py
+++ b/solution.py
@@ -64,7 +64,9 @@
 
     attended = attention(queries, key_cache_table, value_cache_table, filled_lengths)
 
-    own_ids = lax.dynamic_slice_in_dim(request_adapter, group_index * requests, requests)
+    all_ids = request_adapter.reshape(group_count, requests)
+    own_group = jnp.arange(group_count)[:, None] == group_index
+    own_ids = jnp.sum(jnp.where(own_group, all_ids, 0), axis=0)
     id_hot = own_ids[:, None] == jnp.arange(adapter_count)[None, :]
     own_row = jnp.sum(jnp.where(id_hot, adapter_store_row[None, :], 0), axis=1)
     own_dest = own_row // stored_total
@@ -72,19 +74,18 @@
     before = jnp.arange(requests)[:, None] > jnp.arange(requests)[None, :]
     own_order = jnp.sum((same_dest & before).astype(jnp.int32), axis=1)
     own_cell = own_dest * capacity + own_order
-    cell_hot = own_cell[None, :] == jnp.arange(slot_count)[:, None]
+    cell_hot = (own_cell[None, :] == jnp.arange(slot_count)[:, None]).reshape(
+        group_count, capacity, requests
+    )
     outgoing = jnp.einsum(
-        "cb,bf->cf", cell_hot.astype(jnp.bfloat16), attended, preferred_element_type=jnp.float32
+        "dcb,bf->dcf", cell_hot.astype(jnp.bfloat16), attended, preferred_element_type=jnp.float32
     ).astype(jnp.bfloat16)
-    arrived = lax.all_to_all(
-        outgoing.reshape(group_count, capacity, row_width), "dp", 0, 0, tiled=True
-    ).reshape(slot_count, row_width)
+    arrived = lax.all_to_all(outgoing, "dp", 0, 0, tiled=True).reshape(slot_count, row_width)
 
     local_rows = group_index * stored_total + jnp.arange(stored_total)
     holds = adapter_store_row[None, :] == local_rows[:, None]
     local_ids = jnp.sum(jnp.where(holds, jnp.arange(adapter_count)[None, :], 0), axis=1)
     local_factor = jnp.sum(jnp.where(holds, adapter_factor[None, :], 0.0), axis=1)
-    all_ids = request_adapter.reshape(group_count, requests)
     hit = (all_ids[:, :, None] == local_ids[None, None, :]).astype(jnp.bfloat16)
     mine = jnp.sum(hit, axis=2)
     order_in = prefix_count(mine)
@@ -113,9 +114,7 @@
     returned = lax.all_to_all(
         result.reshape(group_count, capacity, row_width), "dp", 0, 0, tiled=True
     ).reshape(slot_count, row_width)
-    adapter_delta = jnp.einsum(
-        "cb,cf->bf", cell_hot.astype(jnp.bfloat16), returned, preferred_element_type=jnp.float32
-    ).astype(jnp.bfloat16)
+    adapter_delta = jnp.take(returned, own_cell, axis=0)
     return (attended, adapter_delta)
 
 

time: 113 us -> 115 us (1.018)
  blocking collectives: 38.3 us -> 0 us
  waiting for transfers between devices: 36.8 us -> 68.6 us
  starting transfers between devices: 23.2 us -> 29 us
  local copies, waits for them, and re-layouts: 5.18 us -> 7.9 us
    all_to_all x1 -> x0, blocking collectives: 38.3 us -> none  [body(): lax.all_to_all(result.reshape(group_count, capacity, row_width), 'dp', 0,...]
    all_to_all x1 -> x2, waiting for transfers between devices: 30.9 us -> 62.6 us  [the longest x1 31.8 us: body(): lax.all_to_all(result.reshape(group_count, capacity, row_width), 'dp', 0,...]
    all_to_all x1 -> x2, starting transfers between devices: 18.7 us -> 24.5 us  [the longest x1 18.6 us: body(): lax.all_to_all(outgoing, 'dp', 0, 0, tiled=True)]
    unnamed x18 -> x16, local copies, waits for them, and re-layouts: 2.1 us -> 3.69 us
    convert_element_type x0 -> x1, local copies, waits for them, and re-layouts: none -> 1.2 us  [body(): outgoing = jnp.einsum('dcb,bf->dcf', cell_hot.astype(jnp.bfloat16), atten...]
  transfers between devices with their start and end apart: 2 -> 3, of which waited for: 2 -> 3; matrix products, arithmetic and copies ran while one was open for 1% -> 2% of each run, Pallas kernels for 0% -> 0%
where the time goes in v2:
time: 115 us; the launch traced here: 114 us
  waiting for transfers between devices  68.6 us (60%)
  starting transfers between devices  29 us (25%)
  local copies, waits for them, and re-layouts  7.9 us (7%)
  matrix products  5.39 us (5%)
  other arithmetic  2.38 us (2%)
    all_to_all x1, waiting for transfers between devices, body(): lax.all_to_all(result.reshape(group_count, capacity, row_width), 'dp', 0,...  31.8 us
    all_to_all x1, waiting for transfers between devices, body(): lax.all_to_all(outgoing, 'dp', 0, 0, tiled=True)  30.9 us
    all_to_all x1, starting transfers between devices, body(): lax.all_to_all(outgoing, 'dp', 0, 0, tiled=True)  18.6 us
    all_to_all x1, waiting for transfers between devices, of_everyone(): lax.all_to_all(copies, axis, split_axis=0, concat_axis=0, tiled=True)  5.96 us
    all_to_all x1, starting transfers between devices, body(): lax.all_to_all(result.reshape(group_count, capacity, row_width), 'dp', 0,...  5.94 us
    all_to_all x1, starting transfers between devices, of_everyone(): lax.all_to_all(copies, axis, split_axis=0, concat_axis=0, tiled=True)  4.47 us
    unnamed x16, local copies, waits for them, and re-layouts  3.69 us
  transfers between devices with their start and end apart: 3, of which 3 were waited for; matrix products, arithmetic and copies ran while one was open for 2% of the time, Pallas kernels for 0%

profile of v2, /device:TPU:6, one launch (start us, length us, event | category | flops | bytes accessed | tf_op | source)
XLA Modules:
  0.0 114.1 jit_solution(18103816100809496587)
XLA Ops:
  0.6 0.0 copy-start
  0.7 0.0 copy-start.4
  0.7 1.1 copy.20
  1.8 0.0 copy-done.4
  1.8 0.1 iota_compare_fusion.4
  1.9 1.9 %fusion.3 = f32[128,8,32]{2,1,0:T(8,128)S(1)} fusion(bf16[128,8,128]{2,1,0:T(8,128)(2,1)S(1)} %bitcast.47, bf16[128,32,128]{2,1,0:T(8,128)(2,1)} %param.10, pred[128,32]{1,0:T(8,128)(4,1)S(1)} %iota_compare_fusion.4), kind=kOutput, calls=%fused_computation.7 | convolution fusion | flops 8454144 | bytes 1445888 | tf_op jit(solution)/shard_map/bkgd,blkd->bkgl/dot_general | solution.py:24
  3.7 0.4 fusion.29
  4.1 0.0 copy-done
  4.1 1.9 %convolution_convert_fusion.1 = bf16[128,8,128]{2,1,0:T(8,128)(2,1)S(1)} fusion(bf16[128,32,128]{2,1,0:T(8,128)(2,1)S(1)} %copy-done, f32[128,8]{1,0:T(8,128)S(1)} %fusion.29, f32[128,8,32]{2,1,0:T(8,128)S(1)} %fusion.3), kind=kOutput, calls=%fused_computation.9 | convolution fusion | flops 8619039 | bytes 1445888 | tf_op jit(solution)/shard_map/bkgl,blkd->bkgd/dot_general | solution.py:32
  6.0 0.0 copy-start.1
  6.0 0.1 reshape.252
  6.1 0.6 copy-done.1
  6.8 0.0 copy-start.2
  6.8 0.1 select_reduce_fusion.1
  6.9 0.6 copy-done.2
  7.5 0.2 select_reduce_fusion
  7.7 0.2 convert_reduce_fusion
  7.9 0.3 convolution_convert_fusion
  8.2 1.2 %copy.18 = bf16[64,4,1024]{2,1,0:T(4,128)(2,1)} copy(bf16[64,4,1024]{2,0,1:T(8,128)(2,1)S(1)} %convolution_convert_fusion) | data formatting | bytes 1048576 | tf_op jit(solution)/shard_map/convert_element_type | solution.py:82
  9.4 18.6 %all-to-all-start = ((bf16[64,4,1024]{2,1,0:T(4,128)(2,1)}), bf16[64,4,1024]{2,1,0:T(4,128)(2,1)S(1)}, u32[]{:S(2)}, u32[]{:S(2)}) async-start(bf16[64,4,1024]{2,1,0:T(4,128)(2,1)} %copy.18), calls=%async_computation | async-start | bytes 1048576 | tf_op jit(solution)/shard_map/all_to_all | solution.py:83
  28.0 0.2 fusion.16
  28.2 0.2 fusion.8
  28.4 0.1 fusion.24
  28.6 0.3 fusion.6
  28.9 0.1 copy.19
  29.0 0.0 copy-start.3
  29.0 0.1 copy.17
  29.0 0.6 copy-done.3
  29.7 0.2 fusion.17
  29.8 0.0 copy-start.5
  29.9 30.9 %all-to-all-done = bf16[64,4,1024]{2,1,0:T(4,128)(2,1)S(1)} async-done(((bf16[64,4,1024]{2,1,0:T(4,128)(2,1)}), bf16[64,4,1024]{2,1,0:T(4,128)(2,1)S(1)}, u32[]{:S(2)}, u32[]{:S(2)}) %all-to-all-start) | async-done | bytes 524320 | tf_op jit(solution)/shard_map/all_to_all | solution.py:83
  60.7 0.1 reshape.253
  60.9 0.0 copy-done.5
  60.9 0.3 fusion.5
  61.2 0.0 copy-start.6
  61.2 0.7 broadcast_in_dim.110
  61.9 4.5 %all-to-all-start.1 = ((f32[8,256,16]{1,2,0:T(8,128)}), f32[8,256,16]{1,2,0:T(8,128)S(1)}, u32[]{:S(2)}, u32[]{:S(2)}) async-start(f32[8,256,16]{1,2,0:T(8,128)} %broadcast_in_dim.110), calls=%async_computation.1 | async-start | bytes 262144 | tf_op jit(solution)/shard_map/all_to_all | solution.py:13
  66.4 0.2 fusion.27
  66.5 6.0 %all-to-all-done.1 = f32[8,256,16]{1,2,0:T(8,128)S(1)} async-done(((f32[8,256,16]{1,2,0:T(8,128)}), f32[8,256,16]{1,2,0:T(8,128)S(1)}, u32[]{:S(2)}, u32[]{:S(2)}) %all-to-all-start.1) | async-done | bytes 131104 | tf_op jit(solution)/shard_map/all_to_all | solution.py:13
  72.5 0.0 copy-done.6
  72.5 0.3 fusion.1
  72.9 1.0 reshape.242
  73.9 5.9 %all-to-all-start.2 = ((bf16[64,4,1024]{2,1,0:T(4,128)(2,1)}), bf16[64,4,1024]{2,1,0:T(4,128)(2,1)S(1)}, u32[]{:S(2)}, u32[]{:S(2)}) async-start(bf16[64,4,1024]{2,1,0:T(4,128)(2,1)} %reshape.242), calls=%async_computation.2 | async-start | bytes 1048576 | tf_op jit(solution)/shard_map/all_to_all | solution.py:114
  79.8 0.8 copy.23
  80.6 31.8 %all-to-all-done.2 = bf16[64,4,1024]{2,1,0:T(4,128)(2,1)S(1)} async-done(((bf16[64,4,1024]{2,1,0:T(4,128)(2,1)}), bf16[64,4,1024]{2,1,0:T(4,128)(2,1)S(1)}, u32[]{:S(2)}, u32[]{:S(2)}) %all-to-all-start.2) | async-done | bytes 524320 | tf_op jit(solution)/shard_map/all_to_all | solution.py:114
  112.3 0.1 reshape.243
  112.5 0.9 gather_fusion
  113.3 0.8 broadcast_select_fusion
  (11 shorter events, 0.1 us)
Async XLA Ops:
  0.6 3.5 %copy-start = (bf16[128,32,128]{2,1,0:T(8,128)(2,1)S(1)}, bf16[128,32,128]{2,1,0:T(8,128)(2,1)}, u32[]{:S(2)}) copy-start(bf16[128,32,128]{2,1,0:T(8,128)(2,1)} %param.11) | copy-start | bytes 3145732
  0.7 1.1 copy-start.4
  6.0 0.8 copy-start.1
  6.8 0.7 copy-start.2
  9.4 51.3 %all-to-all-start = ((bf16[64,4,1024]{2,1,0:T(4,128)(2,1)}), bf16[64,4,1024]{2,1,0:T(4,128)(2,1)S(1)}, u32[]{:S(2)}, u32[]{:S(2)}) async-start(bf16[64,4,1024]{2,1,0:T(4,128)(2,1)} %copy.18), calls=%async_computation | async-start | bytes 1048576 | tf_op jit(solution)/shard_map/all_to_all | solution.py:83
  29.0 0.7 copy-start.3
  29.8 31.0 %copy-start.5 = (bf16[16,16,1024]{2,1,0:T(8,128)(2,1)S(1)}, bf16[16,16,1024]{2,1,0:T(8,128)(2,1)}, u32[]{:S(2)}) copy-start(bf16[16,16,1024]{2,1,0:T(8,128)(2,1)} %param.16) | copy-start | bytes 1572868
  61.2 11.3 %copy-start.6 = (bf16[16,16,1024]{2,1,0:T(8,128)(2,1)S(1)}, bf16[16,16,1024]{2,1,0:T(8,128)(2,1)}, u32[]{:S(2)}) copy-start(bf16[16,16,1024]{2,1,0:T(8,128)(2,1)} %param.17) | copy-start | bytes 1572868
  61.9 10.6 %all-to-all-start.1 = ((f32[8,256,16]{1,2,0:T(8,128)}), f32[8,256,16]{1,2,0:T(8,128)S(1)}, u32[]{:S(2)}, u32[]{:S(2)}) async-start(f32[8,256,16]{1,2,0:T(8,128)} %broadcast_in_dim.110), calls=%async_computation.1 | async-start | bytes 262144 | tf_op jit(solution)/shard_map/all_to_all | solution.py:13
  73.9 38.5 %all-to-all-start.2 = ((bf16[64,4,1024]{2,1,0:T(4,128)(2,1)}), bf16[64,4,1024]{2,1,0:T(4,128)(2,1)S(1)}, u32[]{:S(2)}, u32[]{:S(2)}) async-start(bf16[64,4,1024]{2,1,0:T(4,128)(2,1)} %reshape.242), calls=%async_computation.2 | async-start | bytes 1048576 | tf_op jit(solution)/shard_map/all_to_all | solution.py:114

commit v3 on v1

--- a/solution.py
+++ b/solution.py
@@ -3,9 +3,11 @@
 import jax
 import jax.numpy as jnp
 from jax import lax
+from jax.experimental import pallas as pl
 from jax.sharding import PartitionSpec as P
 
 HEAD_WIDTH = 128
+BLOCK_REQUESTS = 32
 
 
 def of_everyone(value, axis):
@@ -35,6 +37,52 @@
     return attended.astype(jnp.bfloat16).reshape(requests, row_width)
 
 
+def attention_kernel(q_ref, k_ref, v_ref, len_ref, out_ref):
+    block = q_ref.shape[0]
+    heads = q_ref.shape[1] // HEAD_WIDTH
+    length = k_ref.shape[1]
+    width = block * length
+    q = q_ref[...]
+    stacked = jnp.concatenate(
+        [q[:, h * HEAD_WIDTH : (h + 1) * HEAD_WIDTH] for h in range(heads)], axis=0
+    )
+    keys = k_ref[...].reshape(width, HEAD_WIDTH)
+    values = v_ref[...].reshape(width, HEAD_WIDTH)
+    scores = lax.dot_general(
+        stacked, keys, (((1,), (1,)), ((), ())), preferred_element_type=jnp.float32
+    ) * (1.0 / math.sqrt(HEAD_WIDTH))
+    lens = jnp.concatenate([len_ref[...]] * heads, axis=0)
+    row_request = lax.broadcasted_iota(jnp.int32, (heads * block, width), 0) % block
+    col = lax.broadcasted_iota(jnp.int32, (heads * block, width), 1)
+    visible = (col // length == row_request) & (col % length < lens)
+    scores = jnp.where(visible, scores, jnp.float32(-1e30))
+    row_max = jnp.max(scores, axis=-1, keepdims=True)
+    exp_scores = jnp.exp(scores - row_max)
+    weights = (exp_scores / jnp.sum(exp_scores, axis=-1, keepdims=True)).astype(jnp.bfloat16)
+    attended = jnp.dot(weights, values, preferred_element_type=jnp.float32).astype(jnp.bfloat16)
+    for h in range(heads):
+        out_ref[:, h * HEAD_WIDTH : (h + 1) * HEAD_WIDTH] = attended[h * block : (h + 1) * block]
+
+
+def attention_pallas(queries, key_cache_table, value_cache_table, filled_lengths):
+    requests, row_width = queries.shape
+    length = key_cache_table.shape[1]
+    kv_width = key_cache_table.shape[2]
+    block = min(BLOCK_REQUESTS, requests)
+    return pl.pallas_call(
+        attention_kernel,
+        grid=(requests // block,),
+        in_specs=[
+            pl.BlockSpec((block, row_width), lambda i: (i, 0)),
+            pl.BlockSpec((block, length, kv_width), lambda i: (i, 0, 0)),
+            pl.BlockSpec((block, length, kv_width), lambda i: (i, 0, 0)),
+            pl.BlockSpec((block, 1), lambda i: (i, 0)),
+        ],
+        out_specs=pl.BlockSpec((block, row_width), lambda i: (i, 0)),
+        out_shape=jax.ShapeDtypeStruct((requests, row_width), jnp.bfloat16),
+    )(queries, key_cache_table, value_cache_table, filled_lengths.reshape(requests, 1))
+
+
 def prefix_count(mask):
     n = mask.shape[-1]
     earlier = (jnp.arange(n)[:, None] < jnp.arange(n)[None, :]).astype(jnp.bfloat16)
@@ -62,7 +110,10 @@
     stored_total, rank_width = adapter_down_store.shape[0], adapter_down_store.shape[1]
     adapter_count = adapter_store_row.shape[0]
 
-    attended = attention(queries, key_cache_table, value_cache_table, filled_lengths)
+    if key_cache_table.shape[2] == HEAD_WIDTH:
+        attended = attention_pallas(queries, key_cache_table, value_cache_table, filled_lengths)
+    else:
+        attended = attention(queries, key_cache_table, value_cache_table, filled_lengths)
 
     own_ids = lax.dynamic_slice_in_dim(request_adapter, group_index * requests, requests)
     id_hot = own_ids[:, None] == jnp.arange(adapter_count)[None, :]

time: 113 us -> 114 us (level)
  Pallas kernels: 0 us -> 5.08 us
  matrix products: 6.32 us -> 3.5 us
    pallas_call x0 -> x1, Pallas kernels: none -> 5.08 us  [attention_pallas(): pl.pallas_call(attention_kernel, grid=(requests // block,), in_specs=[pl....]
    dot_general x2 -> x0, matrix products: 3.77 us -> none  [the longest x1 1.89 us: attention(): jnp.einsum('bkgl,blkd->bkgd', weights, heads_of_value, preferred_element_...]
where the time goes in v3:
time: 114 us
  blocking collectives  38.3 us (34%)
  waiting for transfers between devices  36.8 us (32%)
  starting transfers between devices  23.2 us (20%)
  local copies, waits for them, and re-layouts  5.08 us (4%)
  Pallas kernels  5.08 us (4%)
  matrix products  3.5 us (3%)
    all_to_all x1, blocking collectives, body(): lax.all_to_all(result.reshape(group_count, capacity, row_width), 'dp', 0,...  38.3 us
    all_to_all x1, waiting for transfers between devices, body(): lax.all_to_all(outgoing.reshape(group_count, capacity, row_width), 'dp',...  30.9 us
    all_to_all x1, starting transfers between devices, body(): lax.all_to_all(outgoing.reshape(group_count, capacity, row_width), 'dp',...  18.7 us
    all_to_all x1, waiting for transfers between devices, of_everyone(): lax.all_to_all(copies, axis, split_axis=0, concat_axis=0, tiled=True)  5.96 us
    pallas_call x1, Pallas kernels, attention_pallas(): pl.pallas_call(attention_kernel, grid=(requests // block,), in_specs=[pl....  5.08 us
    all_to_all x1, starting transfers between devices, of_everyone(): lax.all_to_all(copies, axis, split_axis=0, concat_axis=0, tiled=True)  4.47 us
  transfers between devices with their start and end apart: 2, of which 2 were waited for; matrix products, arithmetic and copies ran while one was open for 1% of the time, Pallas kernels for 0%

profile of v3, /device:TPU:6, one launch (start us, length us, event | category | flops | bytes accessed | tf_op | source)
XLA Modules:
  0.0 113.7 jit_solution(7474588628168417996)
XLA Ops:
  0.6 0.0 copy-start
  0.7 0.0 copy-start.1
  0.7 0.8 dynamic_slice.3
  1.5 0.0 copy-done.1
  1.5 0.2 select_reduce_fusion
  1.7 0.2 convert_reduce_fusion
  1.9 0.0 copy-start.4
  1.9 0.6 copy-done.4
  2.6 0.7 copy.15.len_ref
  3.3 5.1 %shard_map.104 = bf16[128,1024]{1,0:T(8,128)(2,1)} custom-call(bf16[128,1024]{1,0:T(8,128)(2,1)} %q_ref.1, bf16[128,32,128]{2,1,0:T(8,128)(2,1)} %k_ref.1, bf16[128,32,128]{2,1,0:T(8,128)(2,1)} %v_ref.1, s32[128,1]{1,0:T(8,128)} %copy.15.len_ref), custom_call_target="tpu_custom_call" | custom-call | tf_op jit(solution)/shard_map/pallas_call | solution.py:72
  8.4 1.2 %convolution_convert_fusion = bf16[256,1024]{1,0:T(8,128)(2,1)S(1)} fusion(bf16[128,1024]{1,0:T(8,128)(2,1)} %shard_map.104, s32[128]{0:T(128)S(1)} %multiply_add_fusion), kind=kOutput, calls=%fused_computation.2 | convolution fusion | flops 67403776 | bytes 786944 | tf_op jit(solution)/shard_map/cb,bf->cf/dot_general | solution.py:127
  9.6 1.0 reshape.105
  10.6 0.0 copy-start.2
  10.6 18.7 %all-to-all-start = ((bf16[64,4,1024]{2,1,0:T(4,128)(2,1)}), bf16[64,4,1024]{2,1,0:T(4,128)(2,1)S(1)}, u32[]{:S(2)}, u32[]{:S(2)}) async-start(bf16[64,4,1024]{2,1,0:T(4,128)(2,1)} %reshape.105), calls=%async_computation | async-start | bytes 1048576 | tf_op jit(solution)/shard_map/all_to_all | solution.py:130
  29.3 0.2 fusion.10
  29.5 0.0 copy-done.2
  29.5 0.2 fusion.4
  29.7 0.1 fusion.18
  29.9 0.3 fusion.2
  30.2 0.1 copy.17
  30.3 0.0 copy-start.3
  30.3 0.1 copy.16
  30.4 0.6 copy-done.3
  31.0 0.2 fusion.11
  31.2 0.0 copy-start.5
  31.2 30.9 %all-to-all-done = bf16[64,4,1024]{2,1,0:T(4,128)(2,1)S(1)} async-done(((bf16[64,4,1024]{2,1,0:T(4,128)(2,1)}), bf16[64,4,1024]{2,1,0:T(4,128)(2,1)S(1)}, u32[]{:S(2)}, u32[]{:S(2)}) %all-to-all-start) | async-done | bytes 524320 | tf_op jit(solution)/shard_map/all_to_all | solution.py:130
  62.0 0.1 reshape.109
  62.2 0.0 copy-done.5
  62.2 0.3 fusion.1
  62.5 0.7 broadcast_in_dim.42
  63.2 4.5 %all-to-all-start.1 = ((f32[8,256,16]{1,2,0:T(8,128)}), f32[8,256,16]{1,2,0:T(8,128)S(1)}, u32[]{:S(2)}, u32[]{:S(2)}) async-start(f32[8,256,16]{1,2,0:T(8,128)} %broadcast_in_dim.42), calls=%async_computation.1 | async-start | bytes 262144 | tf_op jit(solution)/shard_map/all_to_all | solution.py:15
  67.7 0.2 fusion.20
  67.8 6.0 %all-to-all-done.1 = f32[8,256,16]{1,2,0:T(8,128)S(1)} async-done(((f32[8,256,16]{1,2,0:T(8,128)}), f32[8,256,16]{1,2,0:T(8,128)S(1)}, u32[]{:S(2)}, u32[]{:S(2)}) %all-to-all-start.1) | async-done | bytes 131104 | tf_op jit(solution)/shard_map/all_to_all | solution.py:15
  73.8 0.0 copy-done
  73.8 0.3 fusion
  74.2 0.2 reshape.107
  74.4 38.3 %all_to_all.15 = bf16[64,4,1024]{2,1,0:T(4,128)(2,1)S(1)} all-to-all(bf16[64,4,1024]{2,1,0:T(4,128)(2,1)S(1)} %reshape.107), channel_id=1, replica_groups=mesh['dp'=64,'tensor'=8] {'dp'}, dimensions={0} | all-to-all | bytes 1048576 | tf_op jit(solution)/shard_map/all_to_all | solution.py:164
  112.6 0.1 reshape.108
  112.8 1.0 convolution_convert_fusion.1
  (7 shorter events, 0.1 us)
Async XLA Ops:
  0.6 73.2 %copy-start = (bf16[16,16,1024]{2,1,0:T(8,128)(2,1)S(1)}, bf16[16,16,1024]{2,1,0:T(8,128)(2,1)}, u32[]{:S(2)}) copy-start(bf16[16,16,1024]{2,1,0:T(8,128)(2,1)} %param.17) | copy-start | bytes 1572868
  0.7 0.8 copy-start.1
  1.9 0.7 copy-start.4
  10.6 18.9 %copy-start.2 = (s32[8192]{0:T(1024)S(1)}, s32[8192]{0:T(1024)}, u32[]{:S(2)}) copy-start(s32[8192]{0:T(1024)} %param.13) | copy-start | bytes 98308
  10.6 51.4 %all-to-all-start = ((bf16[64,4,1024]{2,1,0:T(4,128)(2,1)}), bf16[64,4,1024]{2,1,0:T(4,128)(2,1)S(1)}, u32[]{:S(2)}, u32[]{:S(2)}) async-start(bf16[64,4,1024]{2,1,0:T(4,128)(2,1)} %reshape.105), calls=%async_computation | async-start | bytes 1048576 | tf_op jit(solution)/shard_map/all_to_all | solution.py:130
  30.3 0.7 copy-start.3
  31.2 31.0 %copy-start.5 = (bf16[16,16,1024]{2,1,0:T(8,128)(2,1)S(1)}, bf16[16,16,1024]{2,1,0:T(8,128)(2,1)}, u32[]{:S(2)}) copy-start(bf16[16,16,1024]{2,1,0:T(8,128)(2,1)} %param.16) | copy-start | bytes 1572868
  63.2 10.6 %all-to-all-start.1 = ((f32[8,256,16]{1,2,0:T(8,128)}), f32[8,256,16]{1,2,0:T(8,128)S(1)}, u32[]{:S(2)}, u32[]{:S(2)}) async-start(f32[8,256,16]{1,2,0:T(8,128)} %broadcast_in_dim.42), calls=%async_computation.1 | async-start | bytes 262144 | tf_op jit(solution)/shard_map/all_to_all | solution.py:15

commit v4 on v1

--- a/solution.py
+++ b/solution.py
@@ -3,6 +3,7 @@
 import jax
 import jax.numpy as jnp
 from jax import lax
+from jax.experimental import pallas as pl
 from jax.sharding import PartitionSpec as P
 
 HEAD_WIDTH = 128
@@ -33,6 +34,20 @@
         "bkgl,blkd->bkgd", weights, heads_of_value, preferred_element_type=jnp.float32
     )
     return attended.astype(jnp.bfloat16).reshape(requests, row_width)
+
+
+def pack_kernel(hot_ref, rows_ref, out_ref):
+    capacity = out_ref.shape[1]
+    full = jnp.dot(hot_ref[...], rows_ref[...], preferred_element_type=jnp.float32)
+    for d in range(out_ref.shape[0]):
+        out_ref[d] = full[d * capacity : (d + 1) * capacity].astype(out_ref.dtype)
+
+
+def pack_rows(hot, rows, group_count, capacity):
+    return pl.pallas_call(
+        pack_kernel,
+        out_shape=jax.ShapeDtypeStruct((group_count, capacity, rows.shape[1]), rows.dtype),
+    )(hot, rows)
 
 
 def prefix_count(mask):
@@ -73,12 +88,8 @@
     own_order = jnp.sum((same_dest & before).astype(jnp.int32), axis=1)
     own_cell = own_dest * capacity + own_order
     cell_hot = own_cell[None, :] == jnp.arange(slot_count)[:, None]
-    outgoing = jnp.einsum(
-        "cb,bf->cf", cell_hot.astype(jnp.bfloat16), attended, preferred_element_type=jnp.float32
-    ).astype(jnp.bfloat16)
-    arrived = lax.all_to_all(
-        outgoing.reshape(group_count, capacity, row_width), "dp", 0, 0, tiled=True
-    ).reshape(slot_count, row_width)
+    outgoing = pack_rows(cell_hot.astype(jnp.bfloat16), attended, group_count, capacity)
+    arrived = lax.all_to_all(outgoing, "dp", 0, 0, tiled=True).reshape(slot_count, row_width)
 
     local_rows = group_index * stored_total + jnp.arange(stored_total)
     holds = adapter_store_row[None, :] == local_rows[:, None]

time: 113 us -> 114 us (level)
  Pallas kernels: 0 us -> 2.06 us
    pallas_call x0 -> x1, Pallas kernels: none -> 2.06 us  [pack_rows(): pl.pallas_call(pack_kernel, out_shape=jax.ShapeDtypeStruct((group_count,...]
    unnamed x18 -> x16, local copies, waits for them, and re-layouts: 2.1 us -> 2.41 us
where the time goes in v4:
time: 114 us
  blocking collectives  38.3 us (34%)
  waiting for transfers between devices  36.8 us (32%)
  starting transfers between devices  23.2 us (20%)
  matrix products  6.03 us (5%)
  local copies, waits for them, and re-layouts  4.51 us (4%)
  other arithmetic  2.11 us (2%)
  Pallas kernels  2.06 us (2%)
    all_to_all x1, blocking collectives, body(): lax.all_to_all(result.reshape(group_count, capacity, row_width), 'dp', 0,...  38.3 us
    all_to_all x1, waiting for transfers between devices, body(): lax.all_to_all(outgoing, 'dp', 0, 0, tiled=True)  30.9 us
    all_to_all x1, starting transfers between devices, body(): lax.all_to_all(outgoing, 'dp', 0, 0, tiled=True)  18.7 us
    all_to_all x1, waiting for transfers between devices, of_everyone(): lax.all_to_all(copies, axis, split_axis=0, concat_axis=0, tiled=True)  5.96 us
    all_to_all x1, starting transfers between devices, of_everyone(): lax.all_to_all(copies, axis, split_axis=0, concat_axis=0, tiled=True)  4.46 us
    unnamed x16, local copies, waits for them, and re-layouts  2.41 us
  transfers between devices with their start and end apart: 2, of which 2 were waited for; matrix products, arithmetic and copies ran while one was open for 1% of the time, Pallas kernels for 0%

profile of v4, /device:TPU:6, one launch (start us, length us, event | category | flops | bytes accessed | tf_op | source)
XLA Modules:
  0.0 113.8 jit_solution(14077360138733033188)
XLA Ops:
  0.6 0.0 copy-start
  0.7 0.0 copy-start.1
  0.7 0.9 dynamic_slice.3
  1.5 0.0 copy-done.1
  1.5 0.2 select_reduce_fusion
  1.7 0.2 convert_reduce_fusion
  1.9 0.7 fusion.13.hot_ref
  2.6 0.0 copy-start.4
  2.6 1.0 copy.15
  3.6 0.0 copy-done.4
  3.6 0.1 iota_compare_fusion.6
  3.7 1.9 %fusion.3 = f32[128,8,32]{2,1,0:T(8,128)S(1)} fusion(bf16[128,8,128]{2,1,0:T(8,128)(2,1)S(1)} %bitcast.30, bf16[128,32,128]{2,1,0:T(8,128)(2,1)} %param.10, pred[128,32]{1,0:T(8,128)(4,1)S(1)} %iota_compare_fusion.6), kind=kOutput, calls=%fused_computation.5 | convolution fusion | flops 8454144 | bytes 1445888 | tf_op jit(solution)/shard_map/bkgd,blkd->bkgl/dot_general | solution.py:25
  5.6 0.4 fusion.27
  5.9 0.0 copy-done
  5.9 1.9 %convolution_convert_fusion.1 = bf16[128,8,128]{2,1,0:T(8,128)(2,1)S(1)} fusion(bf16[128,32,128]{2,1,0:T(8,128)(2,1)S(1)} %copy-done, f32[128,8]{1,0:T(8,128)S(1)} %fusion.27, f32[128,8,32]{2,1,0:T(8,128)S(1)} %fusion.3), kind=kOutput, calls=%fused_computation.8 | convolution fusion | flops 8619039 | bytes 1445888 | tf_op jit(solution)/shard_map/bkgl,blkd->bkgd/dot_general | solution.py:33
  7.8 0.8 copy.18
  8.6 2.1 %shard_map.104 = bf16[64,4,1024]{2,1,0:T(4,128)(2,1)} custom-call(bf16[256,128]{1,0:T(8,128)(2,1)} %fusion.13.hot_ref, bf16[128,1024]{1,0:T(8,128)(2,1)} %bitcast.31), custom_call_target="tpu_custom_call" | custom-call | tf_op jit(solution)/shard_map/pallas_call | solution.py:47
  10.7 0.0 copy-start.2
  10.7 18.7 %all-to-all-start = ((bf16[64,4,1024]{2,1,0:T(4,128)(2,1)}), bf16[64,4,1024]{2,1,0:T(4,128)(2,1)S(1)}, u32[]{:S(2)}, u32[]{:S(2)}) async-start(bf16[64,4,1024]{2,1,0:T(4,128)(2,1)} %shard_map.104), calls=%async_computation | async-start | bytes 1048576 | tf_op jit(solution)/shard_map/all_to_all | solution.py:92
  29.4 0.2 fusion.16
  29.6 0.0 copy-done.2
  29.6 0.2 fusion.8
  29.8 0.1 fusion.23
  29.9 0.3 fusion.6
  30.2 0.1 copy.14
  30.4 0.0 copy-start.3
  30.4 0.1 copy.13
  30.4 0.6 copy-done.3
  31.0 0.2 fusion.17
  31.2 0.0 copy-start.5
  31.2 30.9 %all-to-all-done = bf16[64,4,1024]{2,1,0:T(4,128)(2,1)S(1)} async-done(((bf16[64,4,1024]{2,1,0:T(4,128)(2,1)}), bf16[64,4,1024]{2,1,0:T(4,128)(2,1)S(1)}, u32[]{:S(2)}, u32[]{:S(2)}) %all-to-all-start) | async-done | bytes 524320 | tf_op jit(solution)/shard_map/all_to_all | solution.py:92
  62.1 0.1 reshape.158
  62.2 0.0 copy-done.5
  62.2 0.3 fusion.5
  62.6 0.0 copy-start.6
  62.6 0.7 broadcast_in_dim.56
  63.3 4.5 %all-to-all-start.1 = ((f32[8,256,16]{1,2,0:T(8,128)}), f32[8,256,16]{1,2,0:T(8,128)S(1)}, u32[]{:S(2)}, u32[]{:S(2)}) async-start(f32[8,256,16]{1,2,0:T(8,128)} %broadcast_in_dim.56), calls=%async_computation.1 | async-start | bytes 262144 | tf_op jit(solution)/shard_map/all_to_all | solution.py:14
  67.7 0.2 fusion.25
  67.9 6.0 %all-to-all-done.1 = f32[8,256,16]{1,2,0:T(8,128)S(1)} async-done(((f32[8,256,16]{1,2,0:T(8,128)}), f32[8,256,16]{1,2,0:T(8,128)S(1)}, u32[]{:S(2)}, u32[]{:S(2)}) %all-to-all-start.1) | async-done | bytes 131104 | tf_op jit(solution)/shard_map/all_to_all | solution.py:14
  73.9 0.0 copy-done.6
  73.9 0.3 fusion.1
  74.2 0.2 reshape.156
  74.4 38.3 %all_to_all.15 = bf16[64,4,1024]{2,1,0:T(4,128)(2,1)S(1)} all-to-all(bf16[64,4,1024]{2,1,0:T(4,128)(2,1)S(1)} %reshape.156), channel_id=1, replica_groups=mesh['dp'=64,'tensor'=8] {'dp'}, dimensions={0} | all-to-all | bytes 1048576 | tf_op jit(solution)/shard_map/all_to_all | solution.py:124
  112.7 0.1 reshape.157
  112.8 1.0 convolution_convert_fusion
  (7 shorter events, 0.1 us)
Async XLA Ops:
  0.6 5.3 %copy-start = (bf16[128,32,128]{2,1,0:T(8,128)(2,1)S(1)}, bf16[128,32,128]{2,1,0:T(8,128)(2,1)}, u32[]{:S(2)}) copy-start(bf16[128,32,128]{2,1,0:T(8,128)(2,1)} %param.11) | copy-start | bytes 3145732
  0.7 0.9 copy-start.1
  2.6 1.0 copy-start.4
  10.7 18.9 %copy-start.2 = (s32[8192]{0:T(1024)S(1)}, s32[8192]{0:T(1024)}, u32[]{:S(2)}) copy-start(s32[8192]{0:T(1024)} %param.13) | copy-start | bytes 98308
  10.7 51.5 %all-to-all-start = ((bf16[64,4,1024]{2,1,0:T(4,128)(2,1)}), bf16[64,4,1024]{2,1,0:T(4,128)(2,1)S(1)}, u32[]{:S(2)}, u32[]{:S(2)}) async-start(bf16[64,4,1024]{2,1,0:T(4,128)(2,1)} %shard_map.104), calls=%async_computation | async-start | bytes 1048576 | tf_op jit(solution)/shard_map/all_to_all | solution.py:92
  30.4 0.7 copy-start.3
  31.2 31.0 %copy-start.5 = (bf16[16,16,1024]{2,1,0:T(8,128)(2,1)S(1)}, bf16[16,16,1024]{2,1,0:T(8,128)(2,1)}, u32[]{:S(2)}) copy-start(bf16[16,16,1024]{2,1,0:T(8,128)(2,1)} %param.16) | copy-start | bytes 1572868
  62.6 11.3 %copy-start.6 = (bf16[16,16,1024]{2,1,0:T(8,128)(2,1)S(1)}, bf16[16,16,1024]{2,1,0:T(8,128)(2,1)}, u32[]{:S(2)}) copy-start(bf16[16,16,1024]{2,1,0:T(8,128)(2,1)} %param.17) | copy-start | bytes 1572868
  63.3 10.6 %all-to-all-start.1 = ((f32[8,256,16]{1,2,0:T(8,128)}), f32[8,256,16]{1,2,0:T(8,128)S(1)}, u32[]{:S(2)}, u32[]{:S(2)}) async-start(f32[8,256,16]{1,2,0:T(8,128)} %broadcast_in_dim.56), calls=%async_computation.1 | async-start | bytes 262144 | tf_op jit(solution)/shard_map/all_to_all | solution.py:14

commit v5 on v1

--- a/solution.py
+++ b/solution.py
@@ -6,6 +6,7 @@
 from jax.sharding import PartitionSpec as P
 
 HEAD_WIDTH = 128
+BLOCK_REQUESTS = 4
 
 
 def of_everyone(value, axis):
@@ -35,6 +36,42 @@
     return attended.astype(jnp.bfloat16).reshape(requests, row_width)
 
 
+def attention_blocked(queries, key_cache_table, value_cache_table, filled_lengths):
+    requests, row_width = queries.shape
+    heads = row_width // HEAD_WIDTH
+    length = key_cache_table.shape[1]
+    block = BLOCK_REQUESTS
+    count = requests // block
+    stacked = (
+        queries.reshape(count, block, heads, HEAD_WIDTH)
+        .transpose(0, 2, 1, 3)
+        .reshape(count, heads * block, HEAD_WIDTH)
+    )
+    keys = key_cache_table.reshape(count, block * length, HEAD_WIDTH)
+    values = value_cache_table.reshape(count, block * length, HEAD_WIDTH)
+    scores = jnp.einsum(
+        "nrd,njd->nrj", stacked, keys, preferred_element_type=jnp.float32
+    ) * (1.0 / math.sqrt(HEAD_WIDTH))
+    row_request = jnp.arange(heads * block) % block
+    col_request = jnp.arange(block * length) // length
+    col_slot = jnp.arange(block * length) % length
+    col_length = jnp.repeat(filled_lengths.reshape(count, block), length, axis=1)
+    visible = (row_request[:, None] == col_request[None, :])[None] & (
+        col_slot[None, None, :] < col_length[:, None, :]
+    )
+    scores = jnp.where(visible, scores, jnp.float32(-1e30))
+    row_max = jnp.max(scores, axis=-1, keepdims=True)
+    exp_scores = jnp.exp(scores - row_max)
+    weights = (exp_scores / jnp.sum(exp_scores, axis=-1, keepdims=True)).astype(jnp.bfloat16)
+    attended = jnp.einsum("nrj,njd->nrd", weights, values, preferred_element_type=jnp.float32)
+    return (
+        attended.astype(jnp.bfloat16)
+        .reshape(count, heads, block, HEAD_WIDTH)
+        .transpose(0, 2, 1, 3)
+        .reshape(requests, row_width)
+    )
+
+
 def prefix_count(mask):
     n = mask.shape[-1]
     earlier = (jnp.arange(n)[:, None] < jnp.arange(n)[None, :]).astype(jnp.bfloat16)
@@ -62,7 +99,10 @@
     stored_total, rank_width = adapter_down_store.shape[0], adapter_down_store.shape[1]
     adapter_count = adapter_store_row.shape[0]
 
-    attended = attention(queries, key_cache_table, value_cache_table, filled_lengths)
+    if key_cache_table.shape[2] == HEAD_WIDTH and requests % BLOCK_REQUESTS == 0:
+        attended = attention_blocked(queries, key_cache_table, value_cache_table, filled_lengths)
+    else:
+        attended = attention(queries, key_cache_table, value_cache_table, filled_lengths)
 
     own_ids = lax.dynamic_slice_in_dim(request_adapter, group_index * requests, requests)
     id_hot = own_ids[:, None] == jnp.arange(adapter_count)[None, :]

time: 113 us -> 113 us (level)
  matrix products: 6.32 us -> 5.03 us
  local copies, waits for them, and re-layouts: 5.18 us -> 6.44 us
    dot_general x2, matrix products: 3.77 us -> 2.47 us  [the longest x1 1.82 us: attention_blocked(): jnp.einsum('nrj,njd->nrd', weights, values, preferred_element_type=jnp.fl...]
    unnamed x18 -> x20, local copies, waits for them, and re-layouts: 2.1 us -> 2.94 us
where the time goes in v5:
time: 113 us; the launch traced here: 112 us
  blocking collectives  38.3 us (34%)
  waiting for transfers between devices  36.8 us (33%)
  starting transfers between devices  23.2 us (21%)
  local copies, waits for them, and re-layouts  6.44 us (6%)
  matrix products  5.03 us (4%)
  other arithmetic  1.46 us (1%)
    all_to_all x1, blocking collectives, body(): lax.all_to_all(result.reshape(group_count, capacity, row_width), 'dp', 0,...  38.3 us
    all_to_all x1, waiting for transfers between devices, body(): lax.all_to_all(outgoing.reshape(group_count, capacity, row_width), 'dp',...  30.9 us
    all_to_all x1, starting transfers between devices, body(): lax.all_to_all(outgoing.reshape(group_count, capacity, row_width), 'dp',...  18.7 us
    all_to_all x1, waiting for transfers between devices, of_everyone(): lax.all_to_all(copies, axis, split_axis=0, concat_axis=0, tiled=True)  5.96 us
    all_to_all x1, starting transfers between devices, of_everyone(): lax.all_to_all(copies, axis, split_axis=0, concat_axis=0, tiled=True)  4.47 us
    unnamed x20, local copies, waits for them, and re-layouts  2.94 us
  transfers between devices with their start and end apart: 2, of which 2 were waited for; matrix products, arithmetic and copies ran while one was open for 1% of the time, Pallas kernels for 0%

profile of v5, /device:TPU:6, one launch (start us, length us, event | category | flops | bytes accessed | tf_op | source)
XLA Modules:
  0.0 112.1 jit_solution(2859019961066317345)
XLA Ops:
  0.6 0.0 copy-start
  0.7 0.0 copy-start.2
  0.7 0.8 dynamic_slice.3
  1.5 0.0 copy-done.2
  1.5 0.2 select_reduce_fusion
  1.8 0.2 convert_reduce_fusion
  1.9 0.0 copy-start.5
  2.0 0.6 copy-done.5
  2.6 0.1 reshape.202
  2.7 0.1 broadcast_in_dim.40
  2.8 0.1 broadcast_in_dim_reshape.2
  2.9 1.0 copy.25
  3.9 0.1 copy.21
  4.0 0.1 broadcast_compare_fusion.1
  4.1 0.0 copy-done
  4.1 0.7 fusion.3
  4.8 0.4 fusion.28
  5.1 0.2 copy-done.6
  5.3 1.8 %convolution_convert_fusion.2 = bf16[32,32,128]{2,1,0:T(8,128)(2,1)S(1)} fusion(bf16[32,128,128]{2,1,0:T(8,128)(2,1)S(1)} %bitcast.52, f32[32,32]{1,0:T(8,128)S(1)} %fusion.28, f32[32,32,128]{2,1,0:T(8,128)S(1)} %fusion.3), kind=kOutput, calls=%fused_computation.9 | convolution fusion | flops 34079872 | bytes 1839104 | tf_op jit(solution)/shard_map/nrj,njd->nrd/dot_general | solution.py:66
  7.3 0.0 copy-start.1
  7.3 0.3 convolution_convert_fusion
  7.6 0.4 copy-done.1
  8.0 1.0 reshape.210
  8.9 18.7 %all-to-all-start = ((bf16[64,4,1024]{2,1,0:T(4,128)(2,1)}), bf16[64,4,1024]{2,1,0:T(4,128)(2,1)S(1)}, u32[]{:S(2)}, u32[]{:S(2)}) async-start(bf16[64,4,1024]{2,1,0:T(4,128)(2,1)} %reshape.210), calls=%async_computation | async-start | bytes 1048576 | tf_op jit(solution)/shard_map/all_to_all | solution.py:119
  27.7 0.2 fusion.15
  27.9 0.0 copy-done.3
  27.9 0.2 fusion.8
  28.1 0.1 fusion.23
  28.2 0.3 fusion.6
  28.5 0.1 copy.24
  28.6 0.0 copy-start.4
  28.6 0.1 copy.23
  28.7 0.6 copy-done.4
  29.3 0.2 fusion.16
  29.5 30.9 %all-to-all-done = bf16[64,4,1024]{2,1,0:T(4,128)(2,1)S(1)} async-done(((bf16[64,4,1024]{2,1,0:T(4,128)(2,1)}), bf16[64,4,1024]{2,1,0:T(4,128)(2,1)S(1)}, u32[]{:S(2)}, u32[]{:S(2)}) %all-to-all-start) | async-done | bytes 524320 | tf_op jit(solution)/shard_map/all_to_all | solution.py:119
  60.4 0.1 reshape.214
  60.5 0.0 copy-done.7
  60.5 0.3 fusion.5
  60.9 0.0 copy-start.8
  60.9 0.7 broadcast_in_dim.50
  61.6 4.5 %all-to-all-start.1 = ((f32[8,256,16]{1,2,0:T(8,128)}), f32[8,256,16]{1,2,0:T(8,128)S(1)}, u32[]{:S(2)}, u32[]{:S(2)}) async-start(f32[8,256,16]{1,2,0:T(8,128)} %broadcast_in_dim.50), calls=%async_computation.1 | async-start | bytes 262144 | tf_op jit(solution)/shard_map/all_to_all | solution.py:14
  66.0 0.2 fusion.25
  66.2 6.0 %all-to-all-done.1 = f32[8,256,16]{1,2,0:T(8,128)S(1)} async-done(((f32[8,256,16]{1,2,0:T(8,128)}), f32[8,256,16]{1,2,0:T(8,128)S(1)}, u32[]{:S(2)}, u32[]{:S(2)}) %all-to-all-start.1) | async-done | bytes 131104 | tf_op jit(solution)/shard_map/all_to_all | solution.py:14
  72.2 0.3 fusion.1
  72.5 0.2 reshape.212
  72.7 38.3 %all_to_all.15 = bf16[64,4,1024]{2,1,0:T(4,128)(2,1)S(1)} all-to-all(bf16[64,4,1024]{2,1,0:T(4,128)(2,1)S(1)} %reshape.212), channel_id=1, replica_groups=mesh['dp'=64,'tensor'=8] {'dp'}, dimensions={0} | all-to-all | bytes 1048576 | tf_op jit(solution)/shard_map/all_to_all | solution.py:153
  111.0 0.1 reshape.213
  111.1 1.0 convolution_convert_fusion.1
  (16 shorter events, 0.2 us)
Async XLA Ops:
  0.6 3.5 %copy-start = (bf16[128,32,128]{2,1,0:T(8,128)(2,1)S(1)}, bf16[128,32,128]{2,1,0:T(8,128)(2,1)}, u32[]{:S(2)}) copy-start(bf16[128,32,128]{2,1,0:T(8,128)(2,1)} %param.10) | copy-start | bytes 3145732
  0.7 0.9 copy-start.2
  1.9 0.7 copy-start.5
  4.1 1.2 %copy-start.6 = (bf16[128,32,128]{2,1,0:T(8,128)(2,1)S(1)}, bf16[128,32,128]{2,1,0:T(8,128)(2,1)}, u32[]{:S(2)}) copy-start(bf16[128,32,128]{2,1,0:T(8,128)(2,1)} %param.11) | copy-start | bytes 3145732
  7.3 0.7 copy-start.1
  8.9 18.9 %copy-start.3 = (s32[8192]{0:T(1024)S(1)}, s32[8192]{0:T(1024)}, u32[]{:S(2)}) copy-start(s32[8192]{0:T(1024)} %param.13) | copy-start | bytes 98308
  8.9 51.4 %all-to-all-start = ((bf16[64,4,1024]{2,1,0:T(4,128)(2,1)}), bf16[64,4,1024]{2,1,0:T(4,128)(2,1)S(1)}, u32[]{:S(2)}, u32[]{:S(2)}) async-start(bf16[64,4,1024]{2,1,0:T(4,128)(2,1)} %reshape.210), calls=%async_computation | async-start | bytes 1048576 | tf_op jit(solution)/shard_map/all_to_all | solution.py:119
  28.6 0.7 copy-start.4
  29.5 31.0 %copy-start.7 = (bf16[16,16,1024]{2,1,0:T(8,128)(2,1)S(1)}, bf16[16,16,1024]{2,1,0:T(8,128)(2,1)}, u32[]{:S(2)}) copy-start(bf16[16,16,1024]{2,1,0:T(8,128)(2,1)} %param.16) | copy-start | bytes 1572868
  60.9 11.3 %copy-start.8 = (bf16[16,16,1024]{2,1,0:T(8,128)(2,1)S(1)}, bf16[16,16,1024]{2,1,0:T(8,128)(2,1)}, u32[]{:S(2)}) copy-start(bf16[16,16,1024]{2,1,0:T(8,128)(2,1)} %param.17) | copy-start | bytes 1572868
  61.6 10.6 %all-to-all-start.1 = ((f32[8,256,16]{1,2,0:T(8,128)}), f32[8,256,16]{1,2,0:T(8,128)S(1)}, u32[]{:S(2)}, u32[]{:S(2)}) async-start(f32[8,256,16]{1,2,0:T(8,128)} %broadcast_in_dim.50), calls=%async_computation.1 | async-start | bytes 262144 | tf_op jit(solution)/shard_map/all_to_all | solution.py:14

commit v6 on v5

--- a/solution.py
+++ b/solution.py
@@ -63,6 +63,7 @@
     row_max = jnp.max(scores, axis=-1, keepdims=True)
     exp_scores = jnp.exp(scores - row_max)
     weights = (exp_scores / jnp.sum(exp_scores, axis=-1, keepdims=True)).astype(jnp.bfloat16)
+    weights = lax.optimization_barrier(weights)
     attended = jnp.einsum("nrj,njd->nrd", weights, values, preferred_element_type=jnp.float32)
     return (
         attended.astype(jnp.bfloat16)

time: 113 us -> 111 us (0.982)
  matrix products: 5.03 us -> 3.73 us
    dot_general x1, matrix products: 1.82 us -> 0.37 us  [attention_blocked(): jnp.einsum('nrj,njd->nrd', weights, values, preferred_element_type=jnp.fl...]
where the time goes in v6:
time: 111 us
  blocking collectives  38.3 us (35%)
  waiting for transfers between devices  36.8 us (33%)
  starting transfers between devices  23.2 us (21%)
  local copies, waits for them, and re-layouts  6.42 us (6%)
  matrix products  3.73 us (3%)
  other arithmetic  1.33 us (1%)
    all_to_all x1, blocking collectives, body(): lax.all_to_all(result.reshape(group_count, capacity, row_width), 'dp', 0,...  38.3 us
    all_to_all x1, waiting for transfers between devices, body(): lax.all_to_all(outgoing.reshape(group_count, capacity, row_width), 'dp',...  30.9 us
    all_to_all x1, starting transfers between devices, body(): lax.all_to_all(outgoing.reshape(group_count, capacity, row_width), 'dp',...  18.7 us
    all_to_all x1, waiting for transfers between devices, of_everyone(): lax.all_to_all(copies, axis, split_axis=0, concat_axis=0, tiled=True)  5.96 us
    all_to_all x1, starting transfers between devices, of_everyone(): lax.all_to_all(copies, axis, split_axis=0, concat_axis=0, tiled=True)  4.47 us
    unnamed x20, local copies, waits for them, and re-layouts  2.91 us
  transfers between devices with their start and end apart: 2, of which 2 were waited for; matrix products, arithmetic and copies ran while one was open for 1% of the time, Pallas kernels for 0%

profile of v6, /device:TPU:6, one launch (start us, length us, event | category | flops | bytes accessed | tf_op | source)
XLA Modules:
  0.0 110.7 jit_solution(2271788364237380925)
XLA Ops:
  0.6 0.0 copy-start
  0.7 0.0 copy-start.3
  0.7 0.8 dynamic_slice.3
  1.5 0.0 copy-done.3
  1.5 0.2 select_reduce_fusion
  1.8 0.2 convert_reduce_fusion
  1.9 0.0 copy-start.6
  2.0 0.6 copy-done.6
  2.6 0.1 reshape.202
  2.7 0.1 broadcast_in_dim.40
  2.8 0.1 broadcast_in_dim_reshape.2
  2.9 1.0 copy.25
  3.9 0.1 copy.21
  4.0 0.1 broadcast_compare_fusion.1
  4.1 0.0 copy-done
  4.1 0.8 fusion.26
  4.9 0.2 divide_convert_fusion
  5.1 0.2 copy-done.1
  5.3 0.4 convolution_convert_fusion.2
  5.7 0.1 copy.22
  5.8 0.0 copy-start.2
  5.8 0.3 convolution_convert_fusion
  6.1 0.4 copy-done.2
  6.5 1.0 reshape.210
  7.5 18.7 %all-to-all-start = ((bf16[64,4,1024]{2,1,0:T(4,128)(2,1)}), bf16[64,4,1024]{2,1,0:T(4,128)(2,1)S(1)}, u32[]{:S(2)}, u32[]{:S(2)}) async-start(bf16[64,4,1024]{2,1,0:T(4,128)(2,1)} %reshape.210), calls=%async_computation | async-start | bytes 1048576 | tf_op jit(solution)/shard_map/all_to_all | solution.py:120
  26.2 0.2 fusion.14
  26.4 0.0 copy-done.4
  26.4 0.2 fusion.8
  26.6 0.1 fusion.22
  26.8 0.3 fusion.6
  27.1 0.1 copy.24
  27.2 0.0 copy-start.5
  27.2 0.1 copy.23
  27.3 0.6 copy-done.5
  27.9 0.2 fusion.15
  28.1 30.9 %all-to-all-done = bf16[64,4,1024]{2,1,0:T(4,128)(2,1)S(1)} async-done(((bf16[64,4,1024]{2,1,0:T(4,128)(2,1)}), bf16[64,4,1024]{2,1,0:T(4,128)(2,1)S(1)}, u32[]{:S(2)}, u32[]{:S(2)}) %all-to-all-start) | async-done | bytes 524320 | tf_op jit(solution)/shard_map/all_to_all | solution.py:120
  58.9 0.1 reshape.214
  59.1 0.3 fusion.5
  59.4 0.0 copy-start.8
  59.4 0.7 broadcast_in_dim.50
  60.1 4.5 %all-to-all-start.1 = ((f32[8,256,16]{1,2,0:T(8,128)}), f32[8,256,16]{1,2,0:T(8,128)S(1)}, u32[]{:S(2)}, u32[]{:S(2)}) async-start(f32[8,256,16]{1,2,0:T(8,128)} %broadcast_in_dim.50), calls=%async_computation.1 | async-start | bytes 262144 | tf_op jit(solution)/shard_map/all_to_all | solution.py:14
  64.6 0.2 fusion.24
  64.8 6.0 %all-to-all-done.1 = f32[8,256,16]{1,2,0:T(8,128)S(1)} async-done(((f32[8,256,16]{1,2,0:T(8,128)}), f32[8,256,16]{1,2,0:T(8,128)S(1)}, u32[]{:S(2)}, u32[]{:S(2)}) %all-to-all-start.1) | async-done | bytes 131104 | tf_op jit(solution)/shard_map/all_to_all | solution.py:14
  70.8 0.3 fusion.1
  71.1 0.2 reshape.212
  71.3 38.3 %all_to_all.15 = bf16[64,4,1024]{2,1,0:T(4,128)(2,1)S(1)} all-to-all(bf16[64,4,1024]{2,1,0:T(4,128)(2,1)S(1)} %reshape.212), channel_id=1, replica_groups=mesh['dp'=64,'tensor'=8] {'dp'}, dimensions={0} | all-to-all | bytes 1048576 | tf_op jit(solution)/shard_map/all_to_all | solution.py:154
  109.6 0.1 reshape.213
  109.7 1.0 convolution_convert_fusion.1
  (16 shorter events, 0.1 us)
Async XLA Ops:
  0.6 3.5 %copy-start = (bf16[128,32,128]{2,1,0:T(8,128)(2,1)S(1)}, bf16[128,32,128]{2,1,0:T(8,128)(2,1)}, u32[]{:S(2)}) copy-start(bf16[128,32,128]{2,1,0:T(8,128)(2,1)} %param.10) | copy-start | bytes 3145732
  0.7 0.9 copy-start.3
  1.9 0.7 copy-start.6
  4.1 1.2 %copy-start.1 = (bf16[128,32,128]{2,1,0:T(8,128)(2,1)S(1)}, bf16[128,32,128]{2,1,0:T(8,128)(2,1)}, u32[]{:S(2)}) copy-start(bf16[128,32,128]{2,1,0:T(8,128)(2,1)} %param.11) | copy-start | bytes 3145732
  5.8 0.7 copy-start.2
  7.5 18.9 %copy-start.4 = (s32[8192]{0:T(1024)S(1)}, s32[8192]{0:T(1024)}, u32[]{:S(2)}) copy-start(s32[8192]{0:T(1024)} %param.13) | copy-start | bytes 98308
  7.5 51.4 %all-to-all-start = ((bf16[64,4,1024]{2,1,0:T(4,128)(2,1)}), bf16[64,4,1024]{2,1,0:T(4,128)(2,1)S(1)}, u32[]{:S(2)}, u32[]{:S(2)}) async-start(bf16[64,4,1024]{2,1,0:T(4,128)(2,1)} %reshape.210), calls=%async_computation | async-start | bytes 1048576 | tf_op jit(solution)/shard_map/all_to_all | solution.py:120
  27.2 0.7 copy-start.5
  28.1 31.0 %copy-start.7 = (bf16[16,16,1024]{2,1,0:T(8,128)(2,1)S(1)}, bf16[16,16,1024]{2,1,0:T(8,128)(2,1)}, u32[]{:S(2)}) copy-start(bf16[16,16,1024]{2,1,0:T(8,128)(2,1)} %param.16) | copy-start | bytes 1572868
  59.4 11.3 %copy-start.8 = (bf16[16,16,1024]{2,1,0:T(8,128)(2,1)S(1)}, bf16[16,16,1024]{2,1,0:T(8,128)(2,1)}, u32[]{:S(2)}) copy-start(bf16[16,16,1024]{2,1,0:T(8,128)(2,1)} %param.17) | copy-start | bytes 1572868
  60.1 10.6 %all-to-all-start.1 = ((f32[8,256,16]{1,2,0:T(8,128)}), f32[8,256,16]{1,2,0:T(8,128)S(1)}, u32[]{:S(2)}, u32[]{:S(2)}) async-start(f32[8,256,16]{1,2,0:T(8,128)} %broadcast_in_dim.50), calls=%async_computation.1 | async-start | bytes 262144 | tf_op jit(solution)/shard_map/all_to_all | solution.py:14

commit v7 on v6

--- a/solution.py
+++ b/solution.py
@@ -113,9 +113,11 @@
     before = jnp.arange(requests)[:, None] > jnp.arange(requests)[None, :]
     own_order = jnp.sum((same_dest & before).astype(jnp.int32), axis=1)
     own_cell = own_dest * capacity + own_order
-    cell_hot = own_cell[None, :] == jnp.arange(slot_count)[:, None]
+    cell_hot = lax.optimization_barrier(
+        (own_cell[None, :] == jnp.arange(slot_count)[:, None]).astype(jnp.bfloat16)
+    )
     outgoing = jnp.einsum(
-        "cb,bf->cf", cell_hot.astype(jnp.bfloat16), attended, preferred_element_type=jnp.float32
+        "cb,bf->cf", cell_hot, attended, preferred_element_type=jnp.float32
     ).astype(jnp.bfloat16)
     arrived = lax.all_to_all(
         outgoing.reshape(group_count, capacity, row_width), "dp", 0, 0, tiled=True
@@ -155,7 +157,7 @@
         result.reshape(group_count, capacity, row_width), "dp", 0, 0, tiled=True
     ).reshape(slot_count, row_width)
     adapter_delta = jnp.einsum(
-        "cb,cf->bf", cell_hot.astype(jnp.bfloat16), returned, preferred_element_type=jnp.float32
+        "cb,cf->bf", cell_hot, returned, preferred_element_type=jnp.float32
     ).astype(jnp.bfloat16)
     return (attended, adapter_delta)
 

time: 111 us -> 111 us (level)
    unnamed x20, local copies, waits for them, and re-layouts: 2.91 us -> 1.32 us
where the time goes in v7:
time: 111 us; the launch traced here: 110 us
  blocking collectives  38.3 us (35%)
  waiting for transfers between devices  36.8 us (33%)
  starting transfers between devices  23.2 us (21%)
  local copies, waits for them, and re-layouts  5.52 us (5%)
  matrix products  3.71 us (3%)
  other arithmetic  2.04 us (2%)
    all_to_all x1, blocking collectives, body(): lax.all_to_all(result.reshape(group_count, capacity, row_width), 'dp', 0,...  38.3 us
    all_to_all x1, waiting for transfers between devices, body(): lax.all_to_all(outgoing.reshape(group_count, capacity, row_width), 'dp',...  30.9 us
    all_to_all x1, starting transfers between devices, body(): lax.all_to_all(outgoing.reshape(group_count, capacity, row_width), 'dp',...  18.7 us
    all_to_all x1, waiting for transfers between devices, of_everyone(): lax.all_to_all(copies, axis, split_axis=0, concat_axis=0, tiled=True)  5.96 us
    all_to_all x1, starting transfers between devices, of_everyone(): lax.all_to_all(copies, axis, split_axis=0, concat_axis=0, tiled=True)  4.47 us
  transfers between devices with their start and end apart: 2, of which 2 were waited for; matrix products, arithmetic and copies ran while one was open for 1% of the time, Pallas kernels for 0%

profile of v7, /device:TPU:6, one launch (start us, length us, event | category | flops | bytes accessed | tf_op | source)
XLA Modules:
  0.0 110.5 jit_solution(3930663075811199720)
XLA Ops:
  0.6 0.0 copy-start
  0.6 0.0 copy-start.3
  0.7 0.9 dynamic_slice.3
  1.6 0.9 select_reduce_fusion
  2.5 0.2 convert_reduce_fusion
  2.7 0.8 reshape.202
  3.5 0.1 broadcast_in_dim.40
  3.6 0.1 broadcast_in_dim_reshape.2
  3.7 0.0 copy-done.3
  3.7 0.1 copy.21
  3.8 0.1 broadcast_compare_fusion.1
  3.9 0.0 copy-done
  3.9 0.8 fusion.25
  4.7 0.2 divide_convert_fusion
  5.0 0.2 copy-done.1
  5.1 0.4 convolution_convert_fusion.2
  5.5 0.1 copy.22
  5.6 0.0 copy-start.2
  5.6 0.3 convolution_convert_fusion
  5.9 0.4 copy-done.2
  6.3 1.0 reshape.210
  7.3 18.7 %all-to-all-start = ((bf16[64,4,1024]{2,1,0:T(4,128)(2,1)}), bf16[64,4,1024]{2,1,0:T(4,128)(2,1)S(1)}, u32[]{:S(2)}, u32[]{:S(2)}) async-start(bf16[64,4,1024]{2,1,0:T(4,128)(2,1)} %reshape.210), calls=%async_computation | async-start | bytes 1048576 | tf_op jit(solution)/shard_map/all_to_all | solution.py:122
  26.1 0.0 copy-done.4
  26.1 0.2 fusion.15
  26.3 0.0 copy-done.5
  26.3 0.2 fusion.8
  26.5 0.1 fusion.21
  26.6 0.3 fusion.6
  26.9 0.1 copy.24
  27.0 0.0 copy-start.6
  27.0 0.1 copy.23
  27.1 0.6 copy-done.6
  27.7 0.2 fusion.16
  27.9 30.9 %all-to-all-done = bf16[64,4,1024]{2,1,0:T(4,128)(2,1)S(1)} async-done(((bf16[64,4,1024]{2,1,0:T(4,128)(2,1)}), bf16[64,4,1024]{2,1,0:T(4,128)(2,1)S(1)}, u32[]{:S(2)}, u32[]{:S(2)}) %all-to-all-start) | async-done | bytes 524320 | tf_op jit(solution)/shard_map/all_to_all | solution.py:122
  58.8 0.1 reshape.214
  58.9 0.0 copy-done.7
  58.9 0.3 fusion.5
  59.2 0.0 copy-start.8
  59.3 0.7 broadcast_in_dim.50
  59.9 4.5 %all-to-all-start.1 = ((f32[8,256,16]{1,2,0:T(8,128)}), f32[8,256,16]{1,2,0:T(8,128)S(1)}, u32[]{:S(2)}, u32[]{:S(2)}) async-start(f32[8,256,16]{1,2,0:T(8,128)} %broadcast_in_dim.50), calls=%async_computation.1 | async-start | bytes 262144 | tf_op jit(solution)/shard_map/all_to_all | solution.py:14
  64.4 0.2 fusion.23
  64.6 6.0 %all-to-all-done.1 = f32[8,256,16]{1,2,0:T(8,128)S(1)} async-done(((f32[8,256,16]{1,2,0:T(8,128)}), f32[8,256,16]{1,2,0:T(8,128)S(1)}, u32[]{:S(2)}, u32[]{:S(2)}) %all-to-all-start.1) | async-done | bytes 131104 | tf_op jit(solution)/shard_map/all_to_all | solution.py:14
  70.6 0.0 copy-done.8
  70.6 0.3 fusion.1
  70.9 0.2 reshape.212
  71.1 38.3 %all_to_all.15 = bf16[64,4,1024]{2,1,0:T(4,128)(2,1)S(1)} all-to-all(bf16[64,4,1024]{2,1,0:T(4,128)(2,1)S(1)} %reshape.212), channel_id=1, replica_groups=mesh['dp'=64,'tensor'=8] {'dp'}, dimensions={0} | all-to-all | bytes 1048576 | tf_op jit(solution)/shard_map/all_to_all | solution.py:156
  109.4 0.1 reshape.213
  109.5 1.0 convolution_convert_fusion.1
  (17 shorter events, 0.2 us)
Async XLA Ops:
  0.6 3.3 %copy-start = (bf16[128,32,128]{2,1,0:T(8,128)(2,1)S(1)}, bf16[128,32,128]{2,1,0:T(8,128)(2,1)}, u32[]{:S(2)}) copy-start(bf16[128,32,128]{2,1,0:T(8,128)(2,1)} %param.10) | copy-start | bytes 3145732
  0.6 3.0 %copy-start.3 = (bf16[128,1024]{1,0:T(8,128)(2,1)S(1)}, bf16[128,1024]{1,0:T(8,128)(2,1)}, u32[]{:S(2)}) copy-start(bf16[128,1024]{1,0:T(8,128)(2,1)} %param.9) | copy-start | bytes 786436
  3.9 1.2 %copy-start.1 = (bf16[128,32,128]{2,1,0:T(8,128)(2,1)S(1)}, bf16[128,32,128]{2,1,0:T(8,128)(2,1)}, u32[]{:S(2)}) copy-start(bf16[128,32,128]{2,1,0:T(8,128)(2,1)} %param.11) | copy-start | bytes 3145732
  5.6 0.7 copy-start.2
  7.3 18.7 %copy-start.4 = (s32[1024]{0:T(1024)S(1)}, s32[1024]{0:T(1024)}, u32[]{:S(2)}) copy-start(s32[1024]{0:T(1024)} %param.14) | copy-start | bytes 12292
  7.3 18.9 %copy-start.5 = (s32[8192]{0:T(1024)S(1)}, s32[8192]{0:T(1024)}, u32[]{:S(2)}) copy-start(s32[8192]{0:T(1024)} %param.13) | copy-start | bytes 98308
  7.3 51.4 %all-to-all-start = ((bf16[64,4,1024]{2,1,0:T(4,128)(2,1)}), bf16[64,4,1024]{2,1,0:T(4,128)(2,1)S(1)}, u32[]{:S(2)}, u32[]{:S(2)}) async-start(bf16[64,4,1024]{2,1,0:T(4,128)(2,1)} %reshape.210), calls=%async_computation | async-start | bytes 1048576 | tf_op jit(solution)/shard_map/all_to_all | solution.py:122
  27.0 0.7 copy-start.6
  27.9 31.0 %copy-start.7 = (bf16[16,16,1024]{2,1,0:T(8,128)(2,1)S(1)}, bf16[16,16,1024]{2,1,0:T(8,128)(2,1)}, u32[]{:S(2)}) copy-start(bf16[16,16,1024]{2,1,0:T(8,128)(2,1)} %param.16) | copy-start | bytes 1572868
  59.2 11.3 %copy-start.8 = (bf16[16,16,1024]{2,1,0:T(8,128)(2,1)S(1)}, bf16[16,16,1024]{2,1,0:T(8,128)(2,1)}, u32[]{:S(2)}) copy-start(bf16[16,16,1024]{2,1,0:T(8,128)(2,1)} %param.17) | copy-start | bytes 1572868
  59.9 10.6 %all-to-all-start.1 = ((f32[8,256,16]{1,2,0:T(8,128)}), f32[8,256,16]{1,2,0:T(8,128)S(1)}, u32[]{:S(2)}, u32[]{:S(2)}) async-start(f32[8,256,16]{1,2,0:T(8,128)} %broadcast_in_dim.50), calls=%async_computation.1 | async-start | bytes 262144 | tf_op jit(solution)/shard_map/all_to_all | solution.py:14

commit v8 on v7

--- a/solution.py
+++ b/solution.py
@@ -113,8 +113,11 @@
     before = jnp.arange(requests)[:, None] > jnp.arange(requests)[None, :]
     own_order = jnp.sum((same_dest & before).astype(jnp.int32), axis=1)
     own_cell = own_dest * capacity + own_order
-    cell_hot = lax.optimization_barrier(
-        (own_cell[None, :] == jnp.arange(slot_count)[:, None]).astype(jnp.bfloat16)
+    cell_hot, request_hot = lax.optimization_barrier(
+        (
+            (own_cell[None, :] == jnp.arange(slot_count)[:, None]).astype(jnp.bfloat16),
+            (own_cell[:, None] == jnp.arange(slot_count)[None, :]).astype(jnp.bfloat16),
+        )
     )
     outgoing = jnp.einsum(
         "cb,bf->cf", cell_hot, attended, preferred_element_type=jnp.float32
@@ -156,9 +159,9 @@
     returned = lax.all_to_all(
         result.reshape(group_count, capacity, row_width), "dp", 0, 0, tiled=True
     ).reshape(slot_count, row_width)
-    adapter_delta = jnp.einsum(
-        "cb,cf->bf", cell_hot, returned, preferred_element_type=jnp.float32
-    ).astype(jnp.bfloat16)
+    adapter_delta = jnp.dot(request_hot, returned, preferred_element_type=jnp.float32).astype(
+        jnp.bfloat16
+    )
     return (attended, adapter_delta)
 
 

time: 111 us -> 111 us (level)
    unnamed x20, local copies, waits for them, and re-layouts: 1.32 us -> 2.81 us
where the time goes in v8:
time: 111 us
  blocking collectives  38.3 us (35%)
  waiting for transfers between devices  36.8 us (33%)
  starting transfers between devices  23.2 us (21%)
  local copies, waits for them, and re-layouts  6.32 us (6%)
  matrix products  3.69 us (3%)
  other arithmetic  1.44 us (1%)
    all_to_all x1, blocking collectives, body(): lax.all_to_all(result.reshape(group_count, capacity, row_width), 'dp', 0,...  38.3 us
    all_to_all x1, waiting for transfers between devices, body(): lax.all_to_all(outgoing.reshape(group_count, capacity, row_width), 'dp',...  30.9 us
    all_to_all x1, starting transfers between devices, body(): lax.all_to_all(outgoing.reshape(group_count, capacity, row_width), 'dp',...  18.7 us
    all_to_all x1, waiting for transfers between devices, of_everyone(): lax.all_to_all(copies, axis, split_axis=0, concat_axis=0, tiled=True)  5.96 us
    all_to_all x1, starting transfers between devices, of_everyone(): lax.all_to_all(copies, axis, split_axis=0, concat_axis=0, tiled=True)  4.47 us
    unnamed x20, local copies, waits for them, and re-layouts  2.81 us
  transfers between devices with their start and end apart: 2, of which 2 were waited for; matrix products, arithmetic and copies ran while one was open for 1% of the time, Pallas kernels for 0%

profile of v8, /device:TPU:6, one launch (start us, length us, event | category | flops | bytes accessed | tf_op | source)
XLA Modules:
  0.0 110.6 jit_solution(8661059067223406799)
XLA Ops:
  0.6 0.0 copy-start
  0.7 0.0 copy-start.3
  0.7 0.8 dynamic_slice.3
  1.5 0.0 copy-done.3
  1.5 0.2 select_reduce_fusion
  1.8 0.2 convert_reduce_fusion
  2.0 0.1 fusion.13
  2.1 1.0 copy.25
  3.1 0.0 copy-start.6
  3.1 0.1 copy.21
  3.2 0.5 copy-done.6
  3.7 0.1 reshape.208
  3.8 0.1 broadcast_in_dim.40
  3.9 0.1 broadcast_in_dim_reshape.2
  4.0 0.1 broadcast_compare_fusion.1
  4.1 0.8 fusion.26
  4.9 0.2 divide_convert_fusion
  5.2 0.2 copy-done.1
  5.4 0.4 convolution_convert_fusion.2
  5.7 0.1 copy.22
  5.8 0.0 copy-start.2
  5.8 0.3 convolution_convert_fusion
  6.1 0.4 copy-done.2
  6.5 1.0 reshape.216
  7.5 18.7 %all-to-all-start = ((bf16[64,4,1024]{2,1,0:T(4,128)(2,1)}), bf16[64,4,1024]{2,1,0:T(4,128)(2,1)S(1)}, u32[]{:S(2)}, u32[]{:S(2)}) async-start(bf16[64,4,1024]{2,1,0:T(4,128)(2,1)} %reshape.216), calls=%async_computation | async-start | bytes 1048576 | tf_op jit(solution)/shard_map/all_to_all | solution.py:125
  26.3 0.2 fusion.16
  26.5 0.2 fusion.8
  26.7 0.1 fusion.22
  26.8 0.3 fusion.6
  27.1 0.1 copy.24
  27.2 0.0 copy-start.5
  27.2 0.1 copy.23
  27.3 0.6 copy-done.5
  27.9 0.2 fusion.17
  28.1 30.9 %all-to-all-done = bf16[64,4,1024]{2,1,0:T(4,128)(2,1)S(1)} async-done(((bf16[64,4,1024]{2,1,0:T(4,128)(2,1)}), bf16[64,4,1024]{2,1,0:T(4,128)(2,1)S(1)}, u32[]{:S(2)}, u32[]{:S(2)}) %all-to-all-start) | async-done | bytes 524320 | tf_op jit(solution)/shard_map/all_to_all | solution.py:125
  59.0 0.1 reshape.220
  59.1 0.3 fusion.5
  59.5 0.0 copy-start.8
  59.5 0.7 broadcast_in_dim.50
  60.1 4.5 %all-to-all-start.1 = ((f32[8,256,16]{1,2,0:T(8,128)}), f32[8,256,16]{1,2,0:T(8,128)S(1)}, u32[]{:S(2)}, u32[]{:S(2)}) async-start(f32[8,256,16]{1,2,0:T(8,128)} %broadcast_in_dim.50), calls=%async_computation.1 | async-start | bytes 262144 | tf_op jit(solution)/shard_map/all_to_all | solution.py:14
  64.6 0.2 fusion.24
  64.8 6.0 %all-to-all-done.1 = f32[8,256,16]{1,2,0:T(8,128)S(1)} async-done(((f32[8,256,16]{1,2,0:T(8,128)}), f32[8,256,16]{1,2,0:T(8,128)S(1)}, u32[]{:S(2)}, u32[]{:S(2)}) %all-to-all-start.1) | async-done | bytes 131104 | tf_op jit(solution)/shard_map/all_to_all | solution.py:14
  70.8 0.0 copy-done.8
  70.8 0.3 fusion.1
  71.1 0.2 reshape.218
  71.3 38.3 %all_to_all.15 = bf16[64,4,1024]{2,1,0:T(4,128)(2,1)S(1)} all-to-all(bf16[64,4,1024]{2,1,0:T(4,128)(2,1)S(1)} %reshape.218), channel_id=1, replica_groups=mesh['dp'=64,'tensor'=8] {'dp'}, dimensions={0} | all-to-all | bytes 1048576 | tf_op jit(solution)/shard_map/all_to_all | solution.py:159
  109.6 0.1 reshape.219
  109.7 0.9 convolution_convert_fusion.1
  (18 shorter events, 0.2 us)
Async XLA Ops:
  0.6 3.5 %copy-start = (bf16[128,32,128]{2,1,0:T(8,128)(2,1)S(1)}, bf16[128,32,128]{2,1,0:T(8,128)(2,1)}, u32[]{:S(2)}) copy-start(bf16[128,32,128]{2,1,0:T(8,128)(2,1)} %param.10) | copy-start | bytes 3145732
  0.7 0.9 copy-start.3
  3.1 0.7 copy-start.6
  4.1 1.2 %copy-start.1 = (bf16[128,32,128]{2,1,0:T(8,128)(2,1)S(1)}, bf16[128,32,128]{2,1,0:T(8,128)(2,1)}, u32[]{:S(2)}) copy-start(bf16[128,32,128]{2,1,0:T(8,128)(2,1)} %param.11) | copy-start | bytes 3145732
  5.8 0.7 copy-start.2
  7.5 18.9 %copy-start.4 = (s32[8192]{0:T(1024)S(1)}, s32[8192]{0:T(1024)}, u32[]{:S(2)}) copy-start(s32[8192]{0:T(1024)} %param.13) | copy-start | bytes 98308
  7.5 51.4 %all-to-all-start = ((bf16[64,4,1024]{2,1,0:T(4,128)(2,1)}), bf16[64,4,1024]{2,1,0:T(4,128)(2,1)S(1)}, u32[]{:S(2)}, u32[]{:S(2)}) async-start(bf16[64,4,1024]{2,1,0:T(4,128)(2,1)} %reshape.216), calls=%async_computation | async-start | bytes 1048576 | tf_op jit(solution)/shard_map/all_to_all | solution.py:125
  27.2 0.7 copy-start.5
  28.1 31.0 %copy-start.7 = (bf16[16,16,1024]{2,1,0:T(8,128)(2,1)S(1)}, bf16[16,16,1024]{2,1,0:T(8,128)(2,1)}, u32[]{:S(2)}) copy-start(bf16[16,16,1024]{2,1,0:T(8,128)(2,1)} %param.16) | copy-start | bytes 1572868
  59.5 11.3 %copy-start.8 = (bf16[16,16,1024]{2,1,0:T(8,128)(2,1)S(1)}, bf16[16,16,1024]{2,1,0:T(8,128)(2,1)}, u32[]{:S(2)}) copy-start(bf16[16,16,1024]{2,1,0:T(8,128)(2,1)} %param.17) | copy-start | bytes 1572868
  60.1 10.6 %all-to-all-start.1 = ((f32[8,256,16]{1,2,0:T(8,128)}), f32[8,256,16]{1,2,0:T(8,128)S(1)}, u32[]{:S(2)}, u32[]{:S(2)}) async-start(f32[8,256,16]{1,2,0:T(8,128)} %broadcast_in_dim.50), calls=%async_computation.1 | async-start | bytes 262144 | tf_op jit(solution)/shard_map/all_to_all | solution.py:14

commit v9 on v7

--- a/solution.py
+++ b/solution.py
@@ -55,7 +55,10 @@
     row_request = jnp.arange(heads * block) % block
     col_request = jnp.arange(block * length) // length
     col_slot = jnp.arange(block * length) % length
-    col_length = jnp.repeat(filled_lengths.reshape(count, block), length, axis=1)
+    col_index = (
+        jnp.arange(count)[:, None] * block + jnp.arange(block * length)[None, :] // length
+    )
+    col_length = jnp.take(filled_lengths, col_index, mode="clip")
     visible = (row_request[:, None] == col_request[None, :])[None] & (
         col_slot[None, None, :] < col_length[:, None, :]
     )

time: 111 us -> 136 us (1.23)
  local copies, waits for them, and re-layouts: 5.52 us -> 30.8 us
    gather x0 -> x1, local copies, waits for them, and re-layouts: none -> 24.7 us  [attention_blocked(): col_length = jnp.take(filled_lengths, col_index, mode='clip')]
    unnamed x20, local copies, waits for them, and re-layouts: 1.32 us -> 2.84 us
where the time goes in v9:
time: 136 us; the launch traced here: 135 us
  blocking collectives  38.3 us (28%)
  waiting for transfers between devices  36.8 us (27%)
  local copies, waits for them, and re-layouts  30.8 us (23%)
  starting transfers between devices  23.2 us (17%)
  matrix products  3.71 us (3%)
  other arithmetic  1.43 us (1%)
    all_to_all x1, blocking collectives, body(): lax.all_to_all(result.reshape(group_count, capacity, row_width), 'dp', 0,...  38.3 us
    all_to_all x1, waiting for transfers between devices, body(): lax.all_to_all(outgoing.reshape(group_count, capacity, row_width), 'dp',...  30.9 us
    gather x1, local copies, waits for them, and re-layouts, attention_blocked(): col_length = jnp.take(filled_lengths, col_index, mode='clip')  24.7 us
    all_to_all x1, starting transfers between devices, body(): lax.all_to_all(outgoing.reshape(group_count, capacity, row_width), 'dp',...  18.7 us
    all_to_all x1, waiting for transfers between devices, of_everyone(): lax.all_to_all(copies, axis, split_axis=0, concat_axis=0, tiled=True)  5.96 us
    all_to_all x1, starting transfers between devices, of_everyone(): lax.all_to_all(copies, axis, split_axis=0, concat_axis=0, tiled=True)  4.47 us
    unnamed x20, local copies, waits for them, and re-layouts  2.84 us
  transfers between devices with their start and end apart: 2, of which 2 were waited for; matrix products, arithmetic and copies ran while one was open for 1% of the time, Pallas kernels for 0%

profile of v9, /device:TPU:6, one launch (start us, length us, event | category | flops | bytes accessed | tf_op | source)
XLA Modules:
  0.0 135.1 jit_solution(15931367968954094492)
XLA Ops:
  0.6 0.0 copy-start
  0.7 0.0 copy-start.4
  0.7 0.8 dynamic_slice.3
  1.6 0.0 copy-done.4
  1.6 0.2 select_reduce_fusion
  1.8 0.2 convert_reduce_fusion
  2.0 1.0 copy.25
  3.0 0.1 copy.21
  3.1 0.0 copy-start.1
  3.1 0.1 bitcast_clamp_fusion
  3.2 0.6 copy-done.1
  3.8 24.7 %gather_fusion = s32[4096]{0:T(1024)S(1)} fusion(s32[128]{0:T(128)S(1)} %copy-done.1, s32[4096]{0:T(1024)S(1)} %bitcast_clamp_fusion), kind=kCustom, calls=%fused_computation | custom fusion | bytes 49152 | tf_op jit(solution)/shard_map/jit(_take)/gather | solution.py:61
  28.5 0.1 bitcast_compare_fusion
  28.6 0.0 copy-done
  28.6 0.8 fusion.25
  29.4 0.2 divide_convert_fusion
  29.6 0.2 copy-done.2
  29.8 0.4 convolution_convert_fusion.2
  30.1 0.1 copy.22
  30.3 0.0 copy-start.3
  30.3 0.3 convolution_convert_fusion
  30.6 0.4 copy-done.3
  31.0 1.0 reshape.276
  32.0 18.7 %all-to-all-start = ((bf16[64,4,1024]{2,1,0:T(4,128)(2,1)}), bf16[64,4,1024]{2,1,0:T(4,128)(2,1)S(1)}, u32[]{:S(2)}, u32[]{:S(2)}) async-start(bf16[64,4,1024]{2,1,0:T(4,128)(2,1)} %reshape.276), calls=%async_computation | async-start | bytes 1048576 | tf_op jit(solution)/shard_map/all_to_all | solution.py:125
  50.7 0.2 fusion.15
  50.9 0.0 copy-done.5
  50.9 0.2 fusion.8
  51.1 0.1 fusion.21
  51.2 0.3 fusion.6
  51.5 0.1 copy.24
  51.6 0.0 copy-start.6
  51.7 0.1 copy.23
  51.7 0.6 copy-done.6
  52.3 0.2 fusion.16
  52.5 30.9 %all-to-all-done = bf16[64,4,1024]{2,1,0:T(4,128)(2,1)S(1)} async-done(((bf16[64,4,1024]{2,1,0:T(4,128)(2,1)}), bf16[64,4,1024]{2,1,0:T(4,128)(2,1)S(1)}, u32[]{:S(2)}, u32[]{:S(2)}) %all-to-all-start) | async-done | bytes 524320 | tf_op jit(solution)/shard_map/all_to_all | solution.py:125
  83.4 0.1 reshape.289
  83.5 0.3 fusion.5
  83.9 0.0 copy-start.8
  83.9 0.7 broadcast_in_dim.45
  84.6 4.5 %all-to-all-start.1 = ((f32[8,256,16]{1,2,0:T(8,128)}), f32[8,256,16]{1,2,0:T(8,128)S(1)}, u32[]{:S(2)}, u32[]{:S(2)}) async-start(f32[8,256,16]{1,2,0:T(8,128)} %broadcast_in_dim.45), calls=%async_computation.1 | async-start | bytes 262144 | tf_op jit(solution)/shard_map/all_to_all | solution.py:14
  89.0 0.2 fusion.23
  89.2 6.0 %all-to-all-done.1 = f32[8,256,16]{1,2,0:T(8,128)S(1)} async-done(((f32[8,256,16]{1,2,0:T(8,128)}), f32[8,256,16]{1,2,0:T(8,128)S(1)}, u32[]{:S(2)}, u32[]{:S(2)}) %all-to-all-start.1) | async-done | bytes 131104 | tf_op jit(solution)/shard_map/all_to_all | solution.py:14
  95.2 0.0 copy-done.8
  95.2 0.3 fusion.1
  95.5 0.2 reshape.278
  95.7 38.3 %all_to_all.15 = bf16[64,4,1024]{2,1,0:T(4,128)(2,1)S(1)} all-to-all(bf16[64,4,1024]{2,1,0:T(4,128)(2,1)S(1)} %reshape.278), channel_id=1, replica_groups=mesh['dp'=64,'tensor'=8] {'dp'}, dimensions={0} | all-to-all | bytes 1048576 | tf_op jit(solution)/shard_map/all_to_all | solution.py:159
  134.0 0.1 reshape.279
  134.1 1.0 convolution_convert_fusion.1
  (17 shorter events, 0.2 us)
Async XLA Ops:
  0.6 27.9 %copy-start = (bf16[128,32,128]{2,1,0:T(8,128)(2,1)S(1)}, bf16[128,32,128]{2,1,0:T(8,128)(2,1)}, u32[]{:S(2)}) copy-start(bf16[128,32,128]{2,1,0:T(8,128)(2,1)} %param.10) | copy-start | bytes 3145732
  0.7 0.9 copy-start.4
  3.1 0.7 copy-start.1
  28.6 1.2 copy-start.2
  30.3 0.7 copy-start.3
  32.0 18.9 %copy-start.5 = (s32[8192]{0:T(1024)S(1)}, s32[8192]{0:T(1024)}, u32[]{:S(2)}) copy-start(s32[8192]{0:T(1024)} %param.13) | copy-start | bytes 98308
  32.0 51.4 %all-to-all-start = ((bf16[64,4,1024]{2,1,0:T(4,128)(2,1)}), bf16[64,4,1024]{2,1,0:T(4,128)(2,1)S(1)}, u32[]{:S(2)}, u32[]{:S(2)}) async-start(bf16[64,4,1024]{2,1,0:T(4,128)(2,1)} %reshape.276), calls=%async_computation | async-start | bytes 1048576 | tf_op jit(solution)/shard_map/all_to_all | solution.py:125
  51.6 0.7 copy-start.6
  52.5 31.0 %copy-start.7 = (bf16[16,16,1024]{2,1,0:T(8,128)(2,1)S(1)}, bf16[16,16,1024]{2,1,0:T(8,128)(2,1)}, u32[]{:S(2)}) copy-start(bf16[16,16,1024]{2,1,0:T(8,128)(2,1)} %param.16) | copy-start | bytes 1572868
  83.9 11.3 %copy-start.8 = (bf16[16,16,1024]{2,1,0:T(8,128)(2,1)S(1)}, bf16[16,16,1024]{2,1,0:T(8,128)(2,1)}, u32[]{:S(2)}) copy-start(bf16[16,16,1024]{2,1,0:T(8,128)(2,1)} %param.17) | copy-start | bytes 1572868
  84.6 10.6 %all-to-all-start.1 = ((f32[8,256,16]{1,2,0:T(8,128)}), f32[8,256,16]{1,2,0:T(8,128)S(1)}, u32[]{:S(2)}, u32[]{:S(2)}) async-start(f32[8,256,16]{1,2,0:T(8,128)} %broadcast_in_dim.45), calls=%async_computation.1 | async-start | bytes 262144 | tf_op jit(solution)/shard_map/all_to_all | solution.py:14

commit v10 on v7

--- a/solution.py
+++ b/solution.py
@@ -106,8 +106,7 @@
         attended = attention(queries, key_cache_table, value_cache_table, filled_lengths)
 
     own_ids = lax.dynamic_slice_in_dim(request_adapter, group_index * requests, requests)
-    id_hot = own_ids[:, None] == jnp.arange(adapter_count)[None, :]
-    own_row = jnp.sum(jnp.where(id_hot, adapter_store_row[None, :], 0), axis=1)
+    own_row = jnp.take(adapter_store_row, own_ids, mode="clip")
     own_dest = own_row // stored_total
     same_dest = own_dest[:, None] == own_dest[None, :]
     before = jnp.arange(requests)[:, None] > jnp.arange(requests)[None, :]

time: 111 us -> 111 us (level)
  no operation moved by 1% of the time
where the time goes in v10:
time: 111 us
  blocking collectives  38.3 us (35%)
  waiting for transfers between devices  36.8 us (33%)
  starting transfers between devices  23.2 us (21%)
  local copies, waits for them, and re-layouts  6.42 us (6%)
  matrix products  3.72 us (3%)
  other arithmetic  1.15 us (1%)
    all_to_all x1, blocking collectives, body(): lax.all_to_all(result.reshape(group_count, capacity, row_width), 'dp', 0,...  38.3 us
    all_to_all x1, waiting for transfers between devices, body(): lax.all_to_all(outgoing.reshape(group_count, capacity, row_width), 'dp',...  30.9 us
    all_to_all x1, starting transfers between devices, body(): lax.all_to_all(outgoing.reshape(group_count, capacity, row_width), 'dp',...  18.7 us
    all_to_all x1, waiting for transfers between devices, of_everyone(): lax.all_to_all(copies, axis, split_axis=0, concat_axis=0, tiled=True)  5.96 us
    all_to_all x1, starting transfers between devices, of_everyone(): lax.all_to_all(copies, axis, split_axis=0, concat_axis=0, tiled=True)  4.47 us
  transfers between devices with their start and end apart: 2, of which 2 were waited for; matrix products, arithmetic and copies ran while one was open for 1% of the time, Pallas kernels for 0%

profile of v10, /device:TPU:6, one launch (start us, length us, event | category | flops | bytes accessed | tf_op | source)
XLA Modules:
  0.0 110.5 jit_solution(11236289239491969399)
XLA Ops:
  0.6 0.0 copy-start
  0.7 0.0 copy-start.1
  0.7 0.8 dynamic_slice.3
  1.6 0.0 copy-start.4
  1.6 1.0 gather_fusion
  2.6 0.2 convert_reduce_fusion
  2.8 0.0 copy-start.7
  2.8 0.6 copy-done.7
  3.4 0.1 reshape.201
  3.5 0.1 broadcast_in_dim.32
  3.6 0.1 broadcast_in_dim_reshape.2
  3.7 0.0 copy-done.4
  3.8 0.1 copy.21
  3.9 0.1 broadcast_compare_fusion.1
  4.0 0.8 fusion.25
  4.8 0.2 divide_convert_fusion
  5.0 0.2 copy-done.2
  5.2 0.4 convolution_convert_fusion.2
  5.6 0.1 copy.22
  5.7 0.0 copy-start.3
  5.7 0.3 convolution_convert_fusion
  6.0 0.4 copy-done.3
  6.4 1.0 reshape.209
  7.4 18.7 %all-to-all-start = ((bf16[64,4,1024]{2,1,0:T(4,128)(2,1)}), bf16[64,4,1024]{2,1,0:T(4,128)(2,1)S(1)}, u32[]{:S(2)}, u32[]{:S(2)}) async-start(bf16[64,4,1024]{2,1,0:T(4,128)(2,1)} %reshape.209), calls=%async_computation | async-start | bytes 1048576 | tf_op jit(solution)/shard_map/all_to_all | solution.py:121
  26.1 0.2 fusion.15
  26.3 0.2 fusion.8
  26.5 0.1 fusion.21
  26.6 0.3 fusion.6
  27.0 0.1 copy.24
  27.1 0.0 copy-start.6
  27.1 0.1 copy.23
  27.1 0.6 copy-done.6
  27.7 0.2 fusion.16
  27.9 30.9 %all-to-all-done = bf16[64,4,1024]{2,1,0:T(4,128)(2,1)S(1)} async-done(((bf16[64,4,1024]{2,1,0:T(4,128)(2,1)}), bf16[64,4,1024]{2,1,0:T(4,128)(2,1)S(1)}, u32[]{:S(2)}, u32[]{:S(2)}) %all-to-all-start) | async-done | bytes 524320 | tf_op jit(solution)/shard_map/all_to_all | solution.py:121
  58.8 0.1 reshape.222
  58.9 0.0 copy-done.8
  58.9 0.3 fusion.5
  59.3 0.0 copy-start.9
  59.3 0.7 broadcast_in_dim.41
  60.0 4.5 %all-to-all-start.1 = ((f32[8,256,16]{1,2,0:T(8,128)}), f32[8,256,16]{1,2,0:T(8,128)S(1)}, u32[]{:S(2)}, u32[]{:S(2)}) async-start(f32[8,256,16]{1,2,0:T(8,128)} %broadcast_in_dim.41), calls=%async_computation.1 | async-start | bytes 262144 | tf_op jit(solution)/shard_map/all_to_all | solution.py:14
  64.5 0.2 fusion.23
  64.6 6.0 %all-to-all-done.1 = f32[8,256,16]{1,2,0:T(8,128)S(1)} async-done(((f32[8,256,16]{1,2,0:T(8,128)}), f32[8,256,16]{1,2,0:T(8,128)S(1)}, u32[]{:S(2)}, u32[]{:S(2)}) %all-to-all-start.1) | async-done | bytes 131104 | tf_op jit(solution)/shard_map/all_to_all | solution.py:14
  70.6 0.0 copy-done.9
  70.6 0.3 fusion.1
  71.0 0.2 reshape.211
  71.2 38.3 %all_to_all.15 = bf16[64,4,1024]{2,1,0:T(4,128)(2,1)S(1)} all-to-all(bf16[64,4,1024]{2,1,0:T(4,128)(2,1)S(1)} %reshape.211), channel_id=1, replica_groups=mesh['dp'=64,'tensor'=8] {'dp'}, dimensions={0} | all-to-all | bytes 1048576 | tf_op jit(solution)/shard_map/all_to_all | solution.py:155
  109.4 0.1 reshape.212
  109.5 1.0 convolution_convert_fusion.1
  (20 shorter events, 0.2 us)
Async XLA Ops:
  0.6 3.3 %copy-start = (bf16[128,32,128]{2,1,0:T(8,128)(2,1)S(1)}, bf16[128,32,128]{2,1,0:T(8,128)(2,1)}, u32[]{:S(2)}) copy-start(bf16[128,32,128]{2,1,0:T(8,128)(2,1)} %param.10) | copy-start | bytes 3145732
  0.7 0.9 copy-start.1
  1.6 2.2 %copy-start.4 = (bf16[128,1024]{1,0:T(8,128)(2,1)S(1)}, bf16[128,1024]{1,0:T(8,128)(2,1)}, u32[]{:S(2)}) copy-start(bf16[128,1024]{1,0:T(8,128)(2,1)} %param.9) | copy-start | bytes 786436
  2.8 0.7 copy-start.7
  4.0 1.2 %copy-start.2 = (bf16[128,32,128]{2,1,0:T(8,128)(2,1)S(1)}, bf16[128,32,128]{2,1,0:T(8,128)(2,1)}, u32[]{:S(2)}) copy-start(bf16[128,32,128]{2,1,0:T(8,128)(2,1)} %param.11) | copy-start | bytes 3145732
  5.7 0.7 copy-start.3
  7.4 18.9 %copy-start.5 = (s32[8192]{0:T(1024)S(1)}, s32[8192]{0:T(1024)}, u32[]{:S(2)}) copy-start(s32[8192]{0:T(1024)} %param.13) | copy-start | bytes 98308
  7.4 51.4 %all-to-all-start = ((bf16[64,4,1024]{2,1,0:T(4,128)(2,1)}), bf16[64,4,1024]{2,1,0:T(4,128)(2,1)S(1)}, u32[]{:S(2)}, u32[]{:S(2)}) async-start(bf16[64,4,1024]{2,1,0:T(4,128)(2,1)} %reshape.209), calls=%async_computation | async-start | bytes 1048576 | tf_op jit(solution)/shard_map/all_to_all | solution.py:121
  27.1 0.7 copy-start.6
  27.9 31.0 %copy-start.8 = (bf16[16,16,1024]{2,1,0:T(8,128)(2,1)S(1)}, bf16[16,16,1024]{2,1,0:T(8,128)(2,1)}, u32[]{:S(2)}) copy-start(bf16[16,16,1024]{2,1,0:T(8,128)(2,1)} %param.16) | copy-start | bytes 1572868
  59.3 11.3 %copy-start.9 = (bf16[16,16,1024]{2,1,0:T(8,128)(2,1)S(1)}, bf16[16,16,1024]{2,1,0:T(8,128)(2,1)}, u32[]{:S(2)}) copy-start(bf16[16,16,1024]{2,1,0:T(8,128)(2,1)} %param.17) | copy-start | bytes 1572868
  60.0 10.6 %all-to-all-start.1 = ((f32[8,256,16]{1,2,0:T(8,128)}), f32[8,256,16]{1,2,0:T(8,128)S(1)}, u32[]{:S(2)}, u32[]{:S(2)}) async-start(f32[8,256,16]{1,2,0:T(8,128)} %broadcast_in_dim.41), calls=%async_computation.1 | async-start | bytes 262144 | tf_op jit(solution)/shard_map/all_to_all | solution.py:14

commit v11 on v10

--- a/solution.py
+++ b/solution.py
@@ -105,7 +105,7 @@
     else:
         attended = attention(queries, key_cache_table, value_cache_table, filled_lengths)
 
-    own_ids = lax.dynamic_slice_in_dim(request_adapter, group_index * requests, requests)
+    own_ids = jnp.take(request_adapter, group_index * requests + jnp.arange(requests), mode="clip")
     own_row = jnp.take(adapter_store_row, own_ids, mode="clip")
     own_dest = own_row // stored_total
     same_dest = own_dest[:, None] == own_dest[None, :]

time: 111 us -> 113 us (1.018)
  local copies, waits for them, and re-layouts: 6.42 us -> 8.59 us
    unnamed x22 -> x20, local copies, waits for them, and re-layouts: 1.94 us -> 3.81 us
    gather x0 -> x1, local copies, waits for them, and re-layouts: none -> 1.15 us  [body(): jnp.take(request_adapter, group_index * requests + jnp.arange(requests),...]
where the time goes in v11:
time: 113 us
  blocking collectives  38.3 us (34%)
  waiting for transfers between devices  36.8 us (33%)
  starting transfers between devices  23.1 us (20%)
  local copies, waits for them, and re-layouts  8.59 us (8%)
  matrix products  3.71 us (3%)
  other arithmetic  1.16 us (1%)
    all_to_all x1, blocking collectives, body(): lax.all_to_all(result.reshape(group_count, capacity, row_width), 'dp', 0,...  38.3 us
    all_to_all x1, waiting for transfers between devices, body(): lax.all_to_all(outgoing.reshape(group_count, capacity, row_width), 'dp',...  30.9 us
    all_to_all x1, starting transfers between devices, body(): lax.all_to_all(outgoing.reshape(group_count, capacity, row_width), 'dp',...  18.6 us
    all_to_all x1, waiting for transfers between devices, of_everyone(): lax.all_to_all(copies, axis, split_axis=0, concat_axis=0, tiled=True)  5.96 us
    all_to_all x1, starting transfers between devices, of_everyone(): lax.all_to_all(copies, axis, split_axis=0, concat_axis=0, tiled=True)  4.47 us
    unnamed x20, local copies, waits for them, and re-layouts  3.81 us
  transfers between devices with their start and end apart: 2, of which 2 were waited for; matrix products, arithmetic and copies ran while one was open for 1% of the time, Pallas kernels for 0%

profile of v11, /device:TPU:6, one launch (start us, length us, event | category | flops | bytes accessed | tf_op | source)
XLA Modules:
  0.0 112.6 jit_solution(2313662584064417343)
XLA Ops:
  0.6 0.0 copy-start
  0.7 1.1 copy.25
  1.8 0.0 copy-start.6
  1.8 0.1 copy.21
  1.9 0.5 copy-done.6
  2.4 0.1 reshape.208
  2.5 0.1 broadcast_in_dim.34
  2.6 0.1 broadcast_in_dim_reshape.2
  2.7 0.1 broadcast_compare_fusion.1
  2.8 0.0 copy-done
  2.8 0.8 fusion.25
  3.6 0.2 divide_convert_fusion
  3.9 0.2 copy-done.3
  4.0 0.4 convolution_convert_fusion.2
  4.4 0.1 copy.22
  4.5 0.0 copy-start.2
  4.5 0.0 copy-start.4
  4.6 0.7 copy-done.2
  5.2 1.1 %gather_fusion = s32[128]{0:T(128)S(1)} fusion(s32[8192]{0:T(1024)S(1)} %copy-done.2, s32[1024]{0:T(1024)S(1)} %pad_clamp_fusion.1), kind=kCustom, calls=%fused_computation | custom fusion | bytes 1536 | tf_op jit(solution)/shard_map/jit(_take)/gather | solution.py:108
  6.4 0.0 copy-start.1
  6.4 0.7 copy-done.1
  7.1 1.0 gather_fusion.1
  8.1 0.2 convert_reduce_fusion
  8.3 0.3 convolution_convert_fusion
  8.6 1.0 reshape.216
  9.6 18.6 %all-to-all-start = ((bf16[64,4,1024]{2,1,0:T(4,128)(2,1)}), bf16[64,4,1024]{2,1,0:T(4,128)(2,1)S(1)}, u32[]{:S(2)}, u32[]{:S(2)}) async-start(bf16[64,4,1024]{2,1,0:T(4,128)(2,1)} %reshape.216), calls=%async_computation | async-start | bytes 1048576 | tf_op jit(solution)/shard_map/all_to_all | solution.py:121
  28.2 0.2 fusion.15
  28.4 0.2 fusion.8
  28.6 0.1 fusion.21
  28.7 0.3 fusion.6
  29.0 0.1 copy.24
  29.1 0.0 copy-start.5
  29.1 0.1 copy.23
  29.2 0.6 copy-done.5
  29.8 0.2 fusion.16
  30.0 30.9 %all-to-all-done = bf16[64,4,1024]{2,1,0:T(4,128)(2,1)S(1)} async-done(((bf16[64,4,1024]{2,1,0:T(4,128)(2,1)}), bf16[64,4,1024]{2,1,0:T(4,128)(2,1)S(1)}, u32[]{:S(2)}, u32[]{:S(2)}) %all-to-all-start) | async-done | bytes 524320 | tf_op jit(solution)/shard_map/all_to_all | solution.py:121
  60.9 0.1 reshape.237
  61.0 0.3 fusion.5
  61.4 0.0 copy-start.8
  61.4 0.7 broadcast_in_dim.43
  62.1 4.5 %all-to-all-start.1 = ((f32[8,256,16]{1,2,0:T(8,128)}), f32[8,256,16]{1,2,0:T(8,128)S(1)}, u32[]{:S(2)}, u32[]{:S(2)}) async-start(f32[8,256,16]{1,2,0:T(8,128)} %broadcast_in_dim.43), calls=%async_computation.1 | async-start | bytes 262144 | tf_op jit(solution)/shard_map/all_to_all | solution.py:14
  66.5 0.2 fusion.23
  66.7 6.0 %all-to-all-done.1 = f32[8,256,16]{1,2,0:T(8,128)S(1)} async-done(((f32[8,256,16]{1,2,0:T(8,128)}), f32[8,256,16]{1,2,0:T(8,128)S(1)}, u32[]{:S(2)}, u32[]{:S(2)}) %all-to-all-start.1) | async-done | bytes 131104 | tf_op jit(solution)/shard_map/all_to_all | solution.py:14
  72.7 0.3 fusion.1
  73.0 0.2 reshape.218
  73.2 38.3 %all_to_all.15 = bf16[64,4,1024]{2,1,0:T(4,128)(2,1)S(1)} all-to-all(bf16[64,4,1024]{2,1,0:T(4,128)(2,1)S(1)} %reshape.218), channel_id=1, replica_groups=mesh['dp'=64,'tensor'=8] {'dp'}, dimensions={0} | all-to-all | bytes 1048576 | tf_op jit(solution)/shard_map/all_to_all | solution.py:155
  111.5 0.1 reshape.219
  111.6 1.0 convolution_convert_fusion.1
  (20 shorter events, 0.2 us)
Async XLA Ops:
  0.6 2.2 %copy-start = (bf16[128,32,128]{2,1,0:T(8,128)(2,1)S(1)}, bf16[128,32,128]{2,1,0:T(8,128)(2,1)}, u32[]{:S(2)}) copy-start(bf16[128,32,128]{2,1,0:T(8,128)(2,1)} %param.10) | copy-start | bytes 3145732
  1.8 0.7 copy-start.6
  2.8 1.2 %copy-start.3 = (bf16[128,32,128]{2,1,0:T(8,128)(2,1)S(1)}, bf16[128,32,128]{2,1,0:T(8,128)(2,1)}, u32[]{:S(2)}) copy-start(bf16[128,32,128]{2,1,0:T(8,128)(2,1)} %param.11) | copy-start | bytes 3145732
  4.5 0.8 copy-start.2
  4.5 3.8 %copy-start.4 = (bf16[16,8,8,128]{3,1,2,0:T(8,128)(2,1)}, bf16[16,8,8,128]{3,1,2,0:T(8,128)(2,1)S(1)}, u32[]{:S(2)}) copy-start(bf16[16,8,8,128]{3,1,2,0:T(8,128)(2,1)S(1)} %copy.28) | copy-start | bytes 786436
  6.4 0.7 copy-start.1
  9.6 51.3 %all-to-all-start = ((bf16[64,4,1024]{2,1,0:T(4,128)(2,1)}), bf16[64,4,1024]{2,1,0:T(4,128)(2,1)S(1)}, u32[]{:S(2)}, u32[]{:S(2)}) async-start(bf16[64,4,1024]{2,1,0:T(4,128)(2,1)} %reshape.216), calls=%async_computation | async-start | bytes 1048576 | tf_op jit(solution)/shard_map/all_to_all | solution.py:121
  29.1 0.7 copy-start.5
  30.0 31.0 %copy-start.7 = (bf16[16,16,1024]{2,1,0:T(8,128)(2,1)S(1)}, bf16[16,16,1024]{2,1,0:T(8,128)(2,1)}, u32[]{:S(2)}) copy-start(bf16[16,16,1024]{2,1,0:T(8,128)(2,1)} %param.16) | copy-start | bytes 1572868
  61.4 11.3 %copy-start.8 = (bf16[16,16,1024]{2,1,0:T(8,128)(2,1)S(1)}, bf16[16,16,1024]{2,1,0:T(8,128)(2,1)}, u32[]{:S(2)}) copy-start(bf16[16,16,1024]{2,1,0:T(8,128)(2,1)} %param.17) | copy-start | bytes 1572868
  62.1 10.6 %all-to-all-start.1 = ((f32[8,256,16]{1,2,0:T(8,128)}), f32[8,256,16]{1,2,0:T(8,128)S(1)}, u32[]{:S(2)}, u32[]{:S(2)}) async-start(f32[8,256,16]{1,2,0:T(8,128)} %broadcast_in_dim.43), calls=%async_computation.1 | async-start | bytes 262144 | tf_op jit(solution)/shard_map/all_to_all | solution.py:14

commit v12 on v10

--- a/solution.py
+++ b/solution.py
@@ -55,7 +55,8 @@
     row_request = jnp.arange(heads * block) % block
     col_request = jnp.arange(block * length) // length
     col_slot = jnp.arange(block * length) % length
-    col_length = jnp.repeat(filled_lengths.reshape(count, block), length, axis=1)
+    lengths = jnp.take(filled_lengths, jnp.arange(requests), mode="clip")
+    col_length = jnp.repeat(lengths.reshape(count, block), length, axis=1)
     visible = (row_request[:, None] == col_request[None, :])[None] & (
         col_slot[None, None, :] < col_length[:, None, :]
     )

time: 111 us -> 112 us (level)
  local copies, waits for them, and re-layouts: 6.42 us -> 7.66 us
    gather x0 -> x1, local copies, waits for them, and re-layouts: none -> 1.22 us  [attention_blocked(): lengths = jnp.take(filled_lengths, jnp.arange(requests), mode='clip')]
where the time goes in v12:
time: 112 us
  blocking collectives  38.3 us (34%)
  waiting for transfers between devices  36.8 us (33%)
  starting transfers between devices  23.2 us (21%)
  local copies, waits for them, and re-layouts  7.66 us (7%)
  matrix products  3.71 us (3%)
  other arithmetic  1.16 us (1%)
    all_to_all x1, blocking collectives, body(): lax.all_to_all(result.reshape(group_count, capacity, row_width), 'dp', 0,...  38.3 us
    all_to_all x1, waiting for transfers between devices, body(): lax.all_to_all(outgoing.reshape(group_count, capacity, row_width), 'dp',...  30.9 us
    all_to_all x1, starting transfers between devices, body(): lax.all_to_all(outgoing.reshape(group_count, capacity, row_width), 'dp',...  18.7 us
    all_to_all x1, waiting for transfers between devices, of_everyone(): lax.all_to_all(copies, axis, split_axis=0, concat_axis=0, tiled=True)  5.96 us
    all_to_all x1, starting transfers between devices, of_everyone(): lax.all_to_all(copies, axis, split_axis=0, concat_axis=0, tiled=True)  4.47 us
  transfers between devices with their start and end apart: 2, of which 2 were waited for; matrix products, arithmetic and copies ran while one was open for 1% of the time, Pallas kernels for 0%

profile of v12, /device:TPU:6, one launch (start us, length us, event | category | flops | bytes accessed | tf_op | source)
XLA Modules:
  0.0 111.8 jit_solution(2345502957774376702)
XLA Ops:
  0.6 0.0 copy-start
  0.7 0.0 copy-start.2
  0.7 0.8 dynamic_slice.3
  1.6 0.0 copy-done.2
  1.6 1.0 gather_fusion.1
  2.5 0.2 convert_reduce_fusion
  2.8 0.0 copy-start.1
  2.8 0.6 copy-done.1
  3.4 1.2 %gather_fusion = s32[128]{0:T(128)S(1)} fusion(s32[128]{0:T(128)S(1)} %copy-done.1, s32[1024]{0:T(1024)S(1)} %pad_clamp_fusion.1), kind=kCustom, calls=%fused_computation | custom fusion | bytes 1536 | tf_op jit(solution)/shard_map/jit(_take)/gather | solution.py:58
  4.7 0.1 reshape.201
  4.8 0.1 broadcast_in_dim.34
  4.9 0.1 broadcast_in_dim_reshape.2
  5.0 0.0 copy-done.5
  5.0 0.1 copy.21
  5.1 0.1 broadcast_compare_fusion.1
  5.2 0.0 copy-done
  5.2 0.8 fusion.25
  6.0 0.2 divide_convert_fusion
  6.3 0.2 copy-done.3
  6.4 0.4 convolution_convert_fusion.2
  6.8 0.1 copy.22
  6.9 0.0 copy-start.4
  6.9 0.3 convolution_convert_fusion
  7.2 0.4 copy-done.4
  7.6 1.0 reshape.209
  8.6 18.7 %all-to-all-start = ((bf16[64,4,1024]{2,1,0:T(4,128)(2,1)}), bf16[64,4,1024]{2,1,0:T(4,128)(2,1)S(1)}, u32[]{:S(2)}, u32[]{:S(2)}) async-start(bf16[64,4,1024]{2,1,0:T(4,128)(2,1)} %reshape.209), calls=%async_computation | async-start | bytes 1048576 | tf_op jit(solution)/shard_map/all_to_all | solution.py:122
  27.4 0.2 fusion.15
  27.6 0.2 fusion.8
  27.8 0.1 fusion.21
  27.9 0.3 fusion.6
  28.2 0.1 copy.24
  28.3 0.0 copy-start.7
  28.3 0.1 copy.23
  28.4 0.6 copy-done.7
  29.0 0.2 fusion.16
  29.2 30.9 %all-to-all-done = bf16[64,4,1024]{2,1,0:T(4,128)(2,1)S(1)} async-done(((bf16[64,4,1024]{2,1,0:T(4,128)(2,1)}), bf16[64,4,1024]{2,1,0:T(4,128)(2,1)S(1)}, u32[]{:S(2)}, u32[]{:S(2)}) %all-to-all-start) | async-done | bytes 524320 | tf_op jit(solution)/shard_map/all_to_all | solution.py:122
  60.1 0.1 reshape.230
  60.2 0.3 fusion.5
  60.6 0.0 copy-start.9
  60.6 0.7 broadcast_in_dim.43
  61.2 4.5 %all-to-all-start.1 = ((f32[8,256,16]{1,2,0:T(8,128)}), f32[8,256,16]{1,2,0:T(8,128)S(1)}, u32[]{:S(2)}, u32[]{:S(2)}) async-start(f32[8,256,16]{1,2,0:T(8,128)} %broadcast_in_dim.43), calls=%async_computation.1 | async-start | bytes 262144 | tf_op jit(solution)/shard_map/all_to_all | solution.py:14
  65.7 0.2 fusion.23
  65.9 6.0 %all-to-all-done.1 = f32[8,256,16]{1,2,0:T(8,128)S(1)} async-done(((f32[8,256,16]{1,2,0:T(8,128)}), f32[8,256,16]{1,2,0:T(8,128)S(1)}, u32[]{:S(2)}, u32[]{:S(2)}) %all-to-all-start.1) | async-done | bytes 131104 | tf_op jit(solution)/shard_map/all_to_all | solution.py:14
  71.9 0.3 fusion.1
  72.2 0.2 reshape.211
  72.4 38.3 %all_to_all.15 = bf16[64,4,1024]{2,1,0:T(4,128)(2,1)S(1)} all-to-all(bf16[64,4,1024]{2,1,0:T(4,128)(2,1)S(1)} %reshape.211), channel_id=1, replica_groups=mesh['dp'=64,'tensor'=8] {'dp'}, dimensions={0} | all-to-all | bytes 1048576 | tf_op jit(solution)/shard_map/all_to_all | solution.py:156
  110.7 0.1 reshape.212
  110.8 1.0 convolution_convert_fusion.1
  (23 shorter events, 0.2 us)
Async XLA Ops:
  0.6 4.6 %copy-start = (bf16[128,32,128]{2,1,0:T(8,128)(2,1)S(1)}, bf16[128,32,128]{2,1,0:T(8,128)(2,1)}, u32[]{:S(2)}) copy-start(bf16[128,32,128]{2,1,0:T(8,128)(2,1)} %param.10) | copy-start | bytes 3145732
  0.7 0.9 copy-start.2
  2.8 0.7 copy-start.1
  3.4 1.5 %copy-start.5 = (bf16[128,1024]{1,0:T(8,128)(2,1)S(1)}, bf16[128,1024]{1,0:T(8,128)(2,1)}, u32[]{:S(2)}) copy-start(bf16[128,1024]{1,0:T(8,128)(2,1)} %param.9) | copy-start | bytes 786436
  5.2 1.2 %copy-start.3 = (bf16[128,32,128]{2,1,0:T(8,128)(2,1)S(1)}, bf16[128,32,128]{2,1,0:T(8,128)(2,1)}, u32[]{:S(2)}) copy-start(bf16[128,32,128]{2,1,0:T(8,128)(2,1)} %param.11) | copy-start | bytes 3145732
  6.9 0.7 copy-start.4
  8.6 18.9 %copy-start.6 = (s32[8192]{0:T(1024)S(1)}, s32[8192]{0:T(1024)}, u32[]{:S(2)}) copy-start(s32[8192]{0:T(1024)} %param.13) | copy-start | bytes 98308
  8.6 51.4 %all-to-all-start = ((bf16[64,4,1024]{2,1,0:T(4,128)(2,1)}), bf16[64,4,1024]{2,1,0:T(4,128)(2,1)S(1)}, u32[]{:S(2)}, u32[]{:S(2)}) async-start(bf16[64,4,1024]{2,1,0:T(4,128)(2,1)} %reshape.209), calls=%async_computation | async-start | bytes 1048576 | tf_op jit(solution)/shard_map/all_to_all | solution.py:122
  28.3 0.7 copy-start.7
  29.2 31.0 %copy-start.8 = (bf16[16,16,1024]{2,1,0:T(8,128)(2,1)S(1)}, bf16[16,16,1024]{2,1,0:T(8,128)(2,1)}, u32[]{:S(2)}) copy-start(bf16[16,16,1024]{2,1,0:T(8,128)(2,1)} %param.16) | copy-start | bytes 1572868
  60.6 11.3 %copy-start.9 = (bf16[16,16,1024]{2,1,0:T(8,128)(2,1)S(1)}, bf16[16,16,1024]{2,1,0:T(8,128)(2,1)}, u32[]{:S(2)}) copy-start(bf16[16,16,1024]{2,1,0:T(8,128)(2,1)} %param.17) | copy-start | bytes 1572868
  61.2 10.6 %all-to-all-start.1 = ((f32[8,256,16]{1,2,0:T(8,128)}), f32[8,256,16]{1,2,0:T(8,128)S(1)}, u32[]{:S(2)}, u32[]{:S(2)}) async-start(f32[8,256,16]{1,2,0:T(8,128)} %broadcast_in_dim.43), calls=%async_computation.1 | async-start | bytes 262144 | tf_op jit(solution)/shard_map/all_to_all | solution.py:14
